TPU v7x, 32 devices: a whole 2x2x4 slice. The times are simulated.
32 devices in a mesh: sky: 8 (over z, x), visit: 4 (over y, core).
Axes of the slice: x: 2, y: 2, z: 4, core: 2. Of those that a mesh axis runs over, the one named last changes fastest.
Arguments:
- tile_image: bfloat16 [4, 256, 128, 128], P('visit', 'sky'), may hold values from -1.1953125 to 1.1953125
- tile_variance: bfloat16 [4, 256, 128, 128], P('visit', 'sky'), may hold values from 0.099609375 to 10
- match_coeffs: bfloat16 [4, 256, 9], P('visit', 'sky'), may hold values from 0.25 to 9
- tile_patch: int32 [4, 256, 1], P('visit', 'sky'), may hold values from 0 to 7; in each aligned block of 32 rows (0 to 31, 32 to 63, ..., all dimensions but the last counted through in order) at most 8 rows name the same one
- tile_offset: int32 [4, 256], P('visit', 'sky'), may hold values from 0 to 63
- row_taps: bfloat16 [9, 41], replicated, may hold values from -1.1953125 to 1.1953125
- col_taps: bfloat16 [9, 41], replicated, may hold values from -1.1953125 to 1.1953125
Outputs:
- coadd_image: float32 [8192, 1024], P('sky', 'visit')
- coadd_variance: float32 [8192, 1024], P('sky', 'visit')
- coadd_psf: float32 [8, 41, 41], P('sky')
Inputs may be any that keep to these rules, and one draw needn't show every extreme that they name: `tile_patch`: among the 32 tiles of one device, at most 8 intersect any one patch.
All inputs are finite; a program needn't handle non-finite values.
Results may differ from a plain program's by a relative error of at most 0.0029.
Values may be sent and summed in bfloat16 or wider, within the bound.
No kernel may reach another device: no remote copies, remote signals or barrier semaphores. Data moves between devices by JAX's collectives and lax.ppermute only.
A program may use at most 64 MiB of HBM per device.

v0:
```python
import jax
import jax.numpy as jnp
from jax import lax
from jax.experimental import pallas as pl
from jax.experimental.pallas import tpu as pltpu
from jax.sharding import PartitionSpec as P

GRID = 8
BASIS = 9
META = 16
EXTRA = 8


weight_floor = 0.5


def band_table(taps, tile):
    span = taps.shape[1]
    offset = jnp.arange(tile)[:, None] - jnp.arange(tile)[None, :] + (span - 1) // 2
    select = (offset[None, :, :] == jnp.arange(span)[:, None, None]).astype(jnp.float32)
    return jnp.einsum("kt,tij->kij", taps.astype(jnp.float32), select).astype(jnp.bfloat16)


def place_tile(out_refs, row, group, sub, contrib):
    tile = contrib.shape[0]
    half = out_refs[0].shape[0]
    per_dev = out_refs[0].shape[2] // tile
    start = pl.multiple_of(row * tile, tile)
    for which, out_ref in enumerate(out_refs):
        for c in range(per_dev):

            @pl.when((sub == c) & (group >= which * half) & (group < (which + 1) * half))
            def _():
                out_ref[group - which * half, pl.ds(start, tile), c * tile:(c + 1) * tile] += contrib


def variance_kernel(row_ref, group_ref, sub_ref, w2_ref, *refs):
    chunks, out_refs = refs[:-2], refs[-2:]
    held = chunks[0].shape[0]
    tile = chunks[0].shape[2]
    for out_ref in out_refs:
        out_ref[...] = jnp.zeros(out_ref.shape, jnp.float32)
    for d, chunk in enumerate(chunks):

        def body(r, carry):
            t = d * held + r
            row = row_ref[t]

            @pl.when(row >= 0)
            def _():
                contrib = w2_ref[t] * chunk[r, :tile, :].astype(jnp.float32)
                place_tile(out_refs, row, group_ref[t], sub_ref[t], contrib)

            return carry

        lax.fori_loop(0, held, body, 0)


def image_kernel(order_ref, count_ref, row_ref, group_ref, sub_ref, w_ref, coef_ref, img_ref,
                 row_side_ref, col_side_ref, extra_ref, *out_refs):
    tile = img_ref.shape[2]
    half, height, width = out_refs[0].shape
    body_rows = height - extra_ref.shape[1]
    for which, out_ref in enumerate(out_refs):
        out_ref[:, :body_rows, :] = jnp.zeros((half, body_rows, width), jnp.float32)
        out_ref[:, body_rows:, :] = extra_ref[which * half:(which + 1) * half]

    def body(p, carry):
        pair = (order_ref[2 * p], order_ref[2 * p + 1])
        both = jnp.concatenate([img_ref[pair[0]], img_ref[pair[1]]], axis=0)
        first = jnp.dot(both, row_side_ref[...], preferred_element_type=jnp.float32)
        blocks = []
        for k in range(BASIS):
            halves = [
                (first[h * tile:(h + 1) * tile, k * tile:(k + 1) * tile]
                 * coef_ref[pair[h] * BASIS + k]).astype(jnp.bfloat16)
                for h in range(2)
            ]
            blocks.append(jnp.concatenate(halves, axis=1))
        scaled = jnp.concatenate(blocks, axis=0)
        matched = jnp.dot(col_side_ref[...], scaled, preferred_element_type=jnp.float32)
        for h in range(2):
            t = pair[h]
            row = row_ref[t]

            @pl.when(row >= 0)
            def _():
                place_tile(out_refs, row, group_ref[t], sub_ref[t],
                           w_ref[t] * matched[:, h * tile:(h + 1) * tile])

        return carry

    lax.fori_loop(0, (count_ref[0] + 1) // 2, body, 0)


def smem():
    return pl.BlockSpec(memory_space=pltpu.SMEM)


def vmem():
    return pl.BlockSpec(memory_space=pltpu.VMEM)


def halves_of(field_shape):
    half = jax.ShapeDtypeStruct((field_shape[0] // 2,) + tuple(field_shape[1:]), jnp.float32)
    return [half, half]


def variance_field(where, w2, chunks, field_shape):
    return pl.pallas_call(
        variance_kernel,
        out_shape=halves_of(field_shape),
        in_specs=[smem()] * 4 + [vmem()] * len(chunks),
        out_specs=[vmem(), vmem()],
    )(*where, w2, *chunks)


def image_field(where, w, coef, images, row_side, col_side, extra, field_shape):
    filled = where[0] >= 0
    order = jnp.argsort(jnp.logical_not(filled), stable=True).astype(jnp.int32)
    count = jnp.sum(filled.astype(jnp.int32))[None]
    return pl.pallas_call(
        image_kernel,
        out_shape=halves_of(field_shape),
        in_specs=[smem()] * 7 + [vmem()] * 4,
        out_specs=[vmem(), vmem()],
        cost_estimate=pl.CostEstimate(
            flops=4 * images.shape[0] * images.shape[2] ** 3 * BASIS,
            transcendentals=0,
            bytes_accessed=images.size * 2 + 4 * (field_shape[0] * field_shape[1] * field_shape[2]),
        ),
    )(order, count, *where, w, coef, images, row_side, col_side, extra)


def bit_reverse(values, bits):
    out = jnp.zeros_like(values)
    for b in range(bits):
        out = out | (((values >> b) & 1) << (bits - 1 - b))
    return out


def reduce_scatter_visit(halves, n_visit):
    bits = n_visit.bit_length() - 1
    keep, send = halves
    for b in range(bits):
        pairs = [(i, i ^ (1 << b)) for i in range(n_visit)]
        field = keep + lax.ppermute(send, "visit", perm=pairs)
        half = field.shape[0] // 2
        keep, send = field[:half], field[half:]
    return field[0]


def shards(tile_image, tile_variance, match_coeffs, tile_patch, tile_offset, row_taps, col_taps):
    n_sky = lax.axis_size("sky")
    n_visit = lax.axis_size("visit")
    images = tile_image[0]
    variance = tile_variance[0]
    coeffs = match_coeffs[0]
    count = images.shape[0]
    tile = images.shape[1]
    held_most = max(2, 2 * count // n_sky)
    positions = GRID * GRID
    per_dev = GRID // n_visit
    dest = tile_patch[0, :, 0]
    offsets = tile_offset[0]
    band_row = band_table(row_taps, tile)
    band_col = band_table(col_taps, tile)
    row_side = band_row.transpose(1, 0, 2).reshape(tile, BASIS * tile)
    col_side = band_col.transpose(2, 0, 1).reshape(tile, BASIS * tile)
    order = jnp.arange(count)
    earlier = (dest[:, None] == dest[None, :]) & (order[None, :] < order[:, None])
    rank = jnp.sum(earlier.astype(jnp.int32), axis=1)
    slot = dest * held_most + rank
    slots_all = n_sky * held_most
    pick = (jnp.arange(slots_all)[:, None] == slot[None, :]).astype(jnp.bfloat16)
    meta_row = jnp.concatenate(
        [coeffs, (offsets + 1).astype(jnp.bfloat16)[:, None],
         jnp.zeros((count, tile - BASIS - 1), jnp.bfloat16)],
        axis=1,
    )
    meta = jnp.concatenate(
        [meta_row[:, None, :], jnp.zeros((count, META - 1, tile), jnp.bfloat16)], axis=1
    )
    var_meta = jnp.concatenate([variance, meta], axis=1)
    taken = (jnp.arange(slots_all)[:, None] == slot[None, :]).astype(jnp.int32)
    source_tile = jnp.sum(taken * order[None, :], axis=1) + count * (1 - jnp.sum(taken, axis=1))

    def gather_slots(values):
        padded = jnp.concatenate([values, jnp.zeros((1,) + values.shape[1:], values.dtype)])
        return jnp.take(padded, source_tile, axis=0, mode="clip").reshape(
            (n_sky, held_most) + values.shape[1:]
        )

    send_vm = gather_slots(var_meta)
    send_im = gather_slots(images)

    part_vm = lax.all_to_all(send_vm, "sky", split_axis=0, concat_axis=0, tiled=True)
    part_vm, send_im = lax.optimization_barrier((part_vm, send_im))
    got_vm = [part_vm.reshape(slots_all, tile + META, tile)]
    got_meta = got_vm[0][:, tile, :].astype(jnp.float32)
    got_coef = got_meta[:, :BASIS]
    place = got_meta[:, BASIS].astype(jnp.int32) - 1
    valid = place >= 0
    mean_var = jnp.mean(got_vm[0][:, :tile, :].astype(jnp.float32), axis=(1, 2))
    weight = jnp.where(valid, 1.0 / jnp.where(valid, mean_var, 1.0), 0.0)
    tile_row = jnp.where(valid, place // GRID, -1)
    tile_col = place % GRID
    bits = n_visit.bit_length() - 1
    me_visit = lax.axis_index("visit")
    where = (tile_row, bit_reverse((tile_col // per_dev) ^ me_visit, bits), tile_col % per_dev)
    psf_part = jnp.sum(weight[:, None] * got_coef, axis=0)
    weight_part = jnp.sum(weight)
    weight_pos = jnp.sum(
        jnp.where(jnp.arange(positions)[:, None] == place[None, :], weight[None, :], 0.0), axis=1
    )
    pos_lanes = weight_pos.reshape(GRID, n_visit, per_dev).transpose(1, 2, 0)
    pos_lanes = jnp.take(pos_lanes, bit_reverse(jnp.arange(n_visit), bits) ^ me_visit, axis=0)
    pos_lanes = jnp.concatenate(
        [pos_lanes, jnp.zeros((n_visit, per_dev, tile - GRID), jnp.float32)], axis=2
    ).reshape(n_visit, 1, per_dev * tile)
    psf_row = jnp.concatenate(
        [psf_part, weight_part[None], jnp.zeros((per_dev * tile - BASIS - 1,), jnp.float32)]
    )
    extra = jnp.concatenate(
        [
            pos_lanes,
            jnp.broadcast_to(psf_row[None, None, :], (n_visit, 1, per_dev * tile)),
            jnp.zeros((n_visit, EXTRA - 2, per_dev * tile), jnp.float32),
        ],
        axis=1,
    )
    var_pos = variance_field(
        where, weight * weight, got_vm, (n_visit, GRID * tile, per_dev * tile)
    )
    var_share = reduce_scatter_visit(var_pos, n_visit)

    part_im = lax.all_to_all(send_im, "sky", split_axis=0, concat_axis=0, tiled=True)
    var_share, part_im = lax.optimization_barrier((var_share, part_im))
    part_im = part_im.reshape(slots_all, tile, tile)
    image_pos = image_field(
        where, weight, got_coef.reshape(slots_all * BASIS), part_im,
        row_side, col_side, extra, (n_visit, GRID * tile + EXTRA, per_dev * tile),
    )
    image_share = reduce_scatter_visit(image_pos, n_visit)

    body_rows = GRID * tile
    pos_weight = image_share[body_rows, :].reshape(per_dev, tile)[:, :GRID]
    denom = jnp.maximum(pos_weight, weight_floor).T
    denom = jnp.broadcast_to(denom[:, None, :, None], (GRID, tile, per_dev, tile))
    denom = denom.reshape(body_rows, per_dev * tile)
    coadd_image = image_share[:body_rows, :] / denom
    coadd_variance = var_share / (denom * denom)

    psf_total = image_share[body_rows + 1, :BASIS]
    weight_total = image_share[body_rows + 1, BASIS]
    share = psf_total / weight_total
    high = lax.Precision.HIGHEST
    coadd_psf = jnp.einsum(
        "k,ka,kb->ab",
        share,
        col_taps.astype(jnp.float32),
        row_taps.astype(jnp.float32),
        precision=high,
    )[None]
    return (coadd_image, coadd_variance, coadd_psf)


def solution(mesh):
    return jax.shard_map(
        shards,
        mesh=mesh,
        in_specs=(
            P("visit", "sky", None, None),
            P("visit", "sky", None, None),
            P("visit", "sky", None),
            P("visit", "sky", None),
            P("visit", "sky"),
            P(),
            P(),
        ),
        out_specs=(P("sky", "visit"), P("sky", "visit"), P("sky", None, None)),
        check_vma=False,
    )
```

profile of v0, /device:TPU:20, one launch (start us, length us, event | category | flops | bytes accessed | tf_op | source)
XLA Modules:
  0.0 181.3 jit_solution(15953914852452718601)
XLA Ops:
  0.6 0.9 convert_reduce_fusion.2
  1.6 0.7 multiply_add_fusion.1
  2.3 0.7 convert_bitcast_fusion
  3.1 0.8 copy.28
  4.2 1.5 maximum_maximum_fusion
  5.8 2.3 %gather_fusion = bf16[64,144,128]{2,1,0:T(8,128)(2,1)} fusion(bf16[33,144,128]{2,1,0:T(8,128)(2,1)S(1)} %concatenate.23, s32[1024]{0:T(1024)S(1)} %pad_clamp_fusion.1), kind=kCustom, calls=%fused_computation | custom fusion | bytes 4718848 | tf_op jit(solution)/shard_map/jit(_take)/gather | solution.py:190
  8.0 6.1 %all-to-all-start = ((bf16[8,8,144,128]{3,2,1,0:T(8,128)(2,1)}), bf16[8,8,144,128]{3,2,1,0:T(8,128)(2,1)S(1)}, u32[]{:S(2)}, u32[]{:S(2)}) async-start(bf16[8,8,144,128]{3,2,1,0:T(8,128)(2,1)} %bitcast.60), calls=%async_computation | async-start | bytes 4718592 | tf_op jit(solution)/shard_map/all_to_all | solution.py:197
  14.2 1.3 concatenate.24
  15.5 2.1 %gather_fusion.1 = bf16[64,128,128]{2,1,0:T(8,128)(2,1)} fusion(bf16[33,128,128]{2,1,0:T(8,128)(2,1)S(1)} %concatenate.24, s32[1024]{0:T(1024)S(1)} %pad_clamp_fusion.1), kind=kCustom, calls=%fused_computation.1 | custom fusion | bytes 4194560 | tf_op jit(solution)/shard_map/jit(_take)/gather | solution.py:190
  17.6 47.1 %all-to-all-done = bf16[8,8,144,128]{3,2,1,0:T(8,128)(2,1)S(1)} async-done(((bf16[8,8,144,128]{3,2,1,0:T(8,128)(2,1)}), bf16[8,8,144,128]{3,2,1,0:T(8,128)(2,1)S(1)}, u32[]{:S(2)}, u32[]{:S(2)}) %all-to-all-start) | async-done | bytes 2359328 | tf_op jit(solution)/shard_map/all_to_all | solution.py:197
  67.3 7.5 %all-to-all-start.1 = ((bf16[8,8,128,128]{3,2,1,0:T(8,128)(2,1)}), bf16[8,8,128,128]{3,2,1,0:T(8,128)(2,1)}, u32[]{:S(2)}, u32[]{:S(2)}) async-start(bf16[8,8,128,128]{3,2,1,0:T(8,128)(2,1)} %bitcast.61), calls=%async_computation.1 | async-start | bytes 4194304 | tf_op jit(solution)/shard_map/all_to_all | solution.py:237
  74.8 1.3 fusion.31
  76.0 7.0 %shard_map.94 = (f32[2,1024,256]{2,1,0:T(8,128)}, f32[2,1024,256]{2,1,0:T(8,128)}) custom-call(s32[64]{0:T(128)} %get-tuple-element.38.row_ref, s32[64]{0:T(128)} %get-tuple-element.44.group_ref, s32[64]{0:T(128)} %get-tuple-element.34.sub_ref, f32[64]{0:T(128)} %mul.54.w2_ref, bf16[64,144,128]{2,1,0:T(8,128)(2,1)} %bitcast.59), custom_call_target="tpu_custom_call" | custom-call | tf_op jit(solution)/shard_map/pallas_call | solution.py:110
  83.1 0.7 fusion.7
  84.1 0.9 copy.35.row_side_ref
  85.0 0.7 fusion.6
  85.8 0.9 copy.36.col_side_ref
  87.9 1.3 copy-done.2
  89.2 2.5 %add.106 = f32[2,1024,256]{2,1,0:T(8,128)S(1)} add(f32[2,1024,256]{2,1,0:T(8,128)} %get-tuple-element.14, f32[2,1024,256]{2,1,0:T(8,128)} %copy-done.2) | non-fusion elementwise | flops 524288 | bytes 6291456 | tf_op jit(solution)/shard_map/add | solution.py:147
  92.7 0.7 reshape.184.coef_ref
  93.5 2.1 %sort.17 = (pred[64]{0:T(512)(128)(4,1)}, s32[64]{0:T(128)}) sort(pred[64]{0:T(512)(128)(4,1)S(1)} %compare_not_fusion, s32[64]{0:T(128)S(1)} %iota.46), dimensions={0}, to_apply=%region_3.4 | sort | flops 384 | bytes 640 | tf_op jit(solution)/shard_map/jit(argsort)/sort | solution.py:120
  95.5 0.7 pad_maximum_fusion
  96.3 0.7 maximum_maximum_fusion.1.extra_ref
  96.9 20.6 %collective-permute-done.1 = f32[1,1024,256]{2,1,0:T(8,128)} collective-permute-done((f32[1,1024,256]{2,1,0:T(8,128)S(1)}, f32[1,1024,256]{2,1,0:T(8,128)}, u32[]{:S(2)}, u32[]{:S(2)}) %collective-permute-start.1) | collective-permute-done | bytes 1048608 | tf_op jit(solution)/shard_map/ppermute | solution.py:147
  117.5 1.4 fusion.9
  119.3 25.6 %shard_map.95 = (f32[2,1032,256]{2,1,0:T(8,128)}, f32[2,1032,256]{2,1,0:T(8,128)}) custom-call(s32[64]{0:T(128)} %get-tuple-element.13.order_ref, s32[1]{0:T(128)} %bitcast.10.count_ref, s32[64]{0:T(128)} %get-tuple-element.38.row_ref, s32[64]{0:T(128)} %get-tuple-element.44.group_ref, s32[64]{0:T(128)} %get-tuple-element.34.sub_ref, f32[64]{0:T(128)} %copy-done.4, ...), custom_call_target="tpu_custom_call" | custom-call | flops 4831838208 | bytes 6324224 | tf_op jit(solution)/shard_map/pallas_call | solution.py:122
  144.9 4.4 %collective-permute-done.2 = f32[2,1032,256]{2,1,0:T(8,128)S(1)} collective-permute-done((f32[2,1032,256]{2,1,0:T(8,128)}, f32[2,1032,256]{2,1,0:T(8,128)S(1)}, u32[]{:S(2)}, u32[]{:S(2)}) %collective-permute-start.2) | collective-permute-done | bytes 2113568 | tf_op jit(solution)/shard_map/ppermute | solution.py:147
  149.3 1.9 %add.111 = f32[2,1032,256]{2,1,0:T(8,128)S(1)} add(f32[2,1032,256]{2,1,0:T(8,128)} %get-tuple-element.18, f32[2,1032,256]{2,1,0:T(8,128)S(1)} %collective-permute-done.2) | non-fusion elementwise | flops 528384 | bytes 6340608 | tf_op jit(solution)/shard_map/add | solution.py:147
  151.9 24.9 %collective-permute-done.3 = f32[1,1032,256]{2,1,0:T(8,128)S(1)} collective-permute-done((f32[1,1032,256]{2,1,0:T(8,128)S(1)}, f32[1,1032,256]{2,1,0:T(8,128)S(1)}, u32[]{:S(2)}, u32[]{:S(2)}) %collective-permute-start.3) | collective-permute-done | bytes 1056800 | tf_op jit(solution)/shard_map/ppermute | solution.py:147
  177.5 0.6 fusion.32
  178.5 0.6 copy.38
  179.5 1.7 fusion.8
  (64 shorter events, 8.1 us)
Async XLA Ops:
  0.6 82.4 %copy-start = (bf16[9,41]{1,0:T(8,128)(2,1)S(1)}, bf16[9,41]{1,0:T(8,128)(2,1)}, u32[]{:S(2)}) copy-start(bf16[9,41]{1,0:T(8,128)(2,1)} %param.12) | copy-start | bytes 2218
  8.0 56.7 %all-to-all-start = ((bf16[8,8,144,128]{3,2,1,0:T(8,128)(2,1)}), bf16[8,8,144,128]{3,2,1,0:T(8,128)(2,1)S(1)}, u32[]{:S(2)}, u32[]{:S(2)}) async-start(bf16[8,8,144,128]{3,2,1,0:T(8,128)(2,1)} %bitcast.60), calls=%async_computation | async-start | bytes 4718592 | tf_op jit(solution)/shard_map/all_to_all | solution.py:197
  64.8 2.5 %copy-start.1 = (bf16[8,8,144,128]{3,2,1,0:T(8,128)(2,1)}, bf16[8,8,144,128]{3,2,1,0:T(8,128)(2,1)S(1)}, u32[]{:S(2)}) copy-start(bf16[8,8,144,128]{3,2,1,0:T(8,128)(2,1)S(1)} %all-to-all-done) | copy-start | bytes 7077892
  66.7 20.2 %copy-start.4 = (f32[64]{0:T(128)}, f32[64]{0:T(128)S(1)}, u32[]{:S(2)}) copy-start(f32[64]{0:T(128)S(1)} %get-tuple-element.33.w_ref) | copy-start | bytes 772
  67.3 52.1 %all-to-all-start.1 = ((bf16[8,8,128,128]{3,2,1,0:T(8,128)(2,1)}), bf16[8,8,128,128]{3,2,1,0:T(8,128)(2,1)}, u32[]{:S(2)}, u32[]{:S(2)}) async-start(bf16[8,8,128,128]{3,2,1,0:T(8,128)(2,1)} %bitcast.61), calls=%async_computation.1 | async-start | bytes 4194304 | tf_op jit(solution)/shard_map/all_to_all | solution.py:237
  76.0 9.0 %copy-start.5 = (bf16[9,41]{1,0:T(8,128)(2,1)S(1)}, bf16[9,41]{1,0:T(8,128)(2,1)}, u32[]{:S(2)}) copy-start(bf16[9,41]{1,0:T(8,128)(2,1)} %param.13) | copy-start | bytes 2218
  83.0 4.8 %collective-permute-start = (f32[2,1024,256]{2,1,0:T(8,128)}, f32[2,1024,256]{2,1,0:T(8,128)S(1)}, u32[]{:S(2)}, u32[]{:S(2)}) collective-permute-start(f32[2,1024,256]{2,1,0:T(8,128)} %get-tuple-element.15), channel_id=1, source_target_pairs={{0,1},{1,0},{2,3},{3,2},{4,5},{5,4},{6,7},{7,6},{8,9},{9,8},{10,11... | collective-permute-start | bytes 6291464 | tf_op jit(solution)/shard_map/ppermute | solution.py:147
  87.9 1.4 copy-start.2
  91.7 1.8 copy-start.3
  91.8 25.7 %collective-permute-start.1 = (f32[1,1024,256]{2,1,0:T(8,128)S(1)}, f32[1,1024,256]{2,1,0:T(8,128)}, u32[]{:S(2)}, u32[]{:S(2)}) collective-permute-start(f32[1,1024,256]{2,1,0:T(8,128)S(1)} %slice.68), channel_id=1, source_target_pairs={{0,2},{1,3},{2,0},{3,1},{4,6},{5,7},{6,4},{7,5},{8,10},{9,11},{10,... | collective-permute-start | bytes 3145736 | tf_op jit(solution)/shard_map/ppermute | solution.py:147
  144.9 4.4 %collective-permute-start.2 = (f32[2,1032,256]{2,1,0:T(8,128)}, f32[2,1032,256]{2,1,0:T(8,128)S(1)}, u32[]{:S(2)}, u32[]{:S(2)}) collective-permute-start(f32[2,1032,256]{2,1,0:T(8,128)} %get-tuple-element.19), channel_id=1, source_target_pairs={{0,1},{1,0},{2,3},{3,2},{4,5},{5,4},{6,7},{7,6},{8,9},{9,8},{10,11... | collective-permute-start | bytes 6340616 | tf_op jit(solution)/shard_map/ppermute | solution.py:147
  151.4 25.4 %collective-permute-start.3 = (f32[1,1032,256]{2,1,0:T(8,128)S(1)}, f32[1,1032,256]{2,1,0:T(8,128)S(1)}, u32[]{:S(2)}, u32[]{:S(2)}) collective-permute-start(f32[1,1032,256]{2,1,0:T(8,128)S(1)} %slice.70), channel_id=1, source_target_pairs={{0,2},{1,3},{2,0},{3,1},{4,6},{5,7},{6,4},{7,5},{8,10},{9,11},{10,... | collective-permute-start | bytes 3170312 | tf_op jit(solution)/shard_map/ppermute | solution.py:147
where the time goes:
time: 182 us; the launch traced here: 181 us
  waiting for transfers between devices  97.4 us (54%)
  Pallas kernels  32.6 us (18%)
  other arithmetic  20 us (11%)
  starting transfers between devices  14.8 us (8%)
  local copies, waits for them, and re-layouts  14 us (8%)
    ppermute x4, waiting for transfers between devices, reduce_scatter_visit(): field = keep + lax.ppermute(send, 'visit', perm=pairs)  49.9 us
    all_to_all x1, waiting for transfers between devices, shards(): lax.all_to_all(send_vm, 'sky', split_axis=0, concat_axis=0, tiled=True)  47.1 us
    pallas_call x1, Pallas kernels, image_field(): pl.pallas_call(image_kernel, out_shape=halves_of(field_shape), in_specs=[...  25.6 us
    all_to_all x1, starting transfers between devices, shards(): lax.all_to_all(send_im, 'sky', split_axis=0, concat_axis=0, tiled=True)  7.52 us
    pallas_call x1, Pallas kernels, variance_field(): pl.pallas_call(variance_kernel, out_shape=halves_of(field_shape), in_spec...  7 us
    all_to_all x1, starting transfers between devices, shards(): lax.all_to_all(send_vm, 'sky', split_axis=0, concat_axis=0, tiled=True)  6.14 us
    add x3, other arithmetic, reduce_scatter_visit(): field = keep + lax.ppermute(send, 'visit', perm=pairs)  4.56 us
    gather x2, local copies, waits for them, and re-layouts, gather_slots(): jnp.take(padded, source_tile, axis=0, mode='clip')  4.4 us
  transfers between devices with their start and end apart: 6, of which 5 were waited for; matrix products, arithmetic and copies ran while one was open for 10% of the time, Pallas kernels for 4%

commit v1 on v0

--- a/solution.py
+++ b/solution.py
@@ -57,13 +57,17 @@
 
 
 def image_kernel(order_ref, count_ref, row_ref, group_ref, sub_ref, w_ref, coef_ref, img_ref,
-                 row_side_ref, col_side_ref, extra_ref, *out_refs):
+                 row_side_ref, col_side_ref, extra_ref, *refs):
     tile = img_ref.shape[2]
+    out_refs = refs[-2:]
     half, height, width = out_refs[0].shape
     body_rows = height - extra_ref.shape[1]
     for which, out_ref in enumerate(out_refs):
-        out_ref[:, :body_rows, :] = jnp.zeros((half, body_rows, width), jnp.float32)
-        out_ref[:, body_rows:, :] = extra_ref[which * half:(which + 1) * half]
+        if len(refs) == 4:
+            out_ref[...] = refs[which][...]
+        else:
+            out_ref[:, :body_rows, :] = jnp.zeros((half, body_rows, width), jnp.float32)
+            out_ref[:, body_rows:, :] = extra_ref[which * half:(which + 1) * half]
 
     def body(p, carry):
         pair = (order_ref[2 * p], order_ref[2 * p + 1])
@@ -115,21 +119,22 @@
     )(*where, w2, *chunks)
 
 
-def image_field(where, w, coef, images, row_side, col_side, extra, field_shape):
+def image_field(where, w, coef, images, row_side, col_side, extra, field_shape, field=()):
     filled = where[0] >= 0
     order = jnp.argsort(jnp.logical_not(filled), stable=True).astype(jnp.int32)
     count = jnp.sum(filled.astype(jnp.int32))[None]
     return pl.pallas_call(
         image_kernel,
         out_shape=halves_of(field_shape),
-        in_specs=[smem()] * 7 + [vmem()] * 4,
+        in_specs=[smem()] * 7 + [vmem()] * (4 + len(field)),
         out_specs=[vmem(), vmem()],
+        input_output_aliases={11 + i: i for i in range(len(field))},
         cost_estimate=pl.CostEstimate(
             flops=4 * images.shape[0] * images.shape[2] ** 3 * BASIS,
             transcendentals=0,
             bytes_accessed=images.size * 2 + 4 * (field_shape[0] * field_shape[1] * field_shape[2]),
         ),
-    )(order, count, *where, w, coef, images, row_side, col_side, extra)
+    )(order, count, *where, w, coef, images, row_side, col_side, extra, *field)
 
 
 def bit_reverse(values, bits):
@@ -234,13 +239,24 @@
     )
     var_share = reduce_scatter_visit(var_pos, n_visit)
 
-    part_im = lax.all_to_all(send_im, "sky", split_axis=0, concat_axis=0, tiled=True)
-    var_share, part_im = lax.optimization_barrier((var_share, part_im))
-    part_im = part_im.reshape(slots_all, tile, tile)
-    image_pos = image_field(
-        where, weight, got_coef.reshape(slots_all * BASIS), part_im,
-        row_side, col_side, extra, (n_visit, GRID * tile + EXTRA, per_dev * tile),
-    )
+    low = held_most // 2
+    part_a = lax.all_to_all(send_im[:, :low], "sky", split_axis=0, concat_axis=0, tiled=True)
+    part_a, send_b = lax.optimization_barrier((part_a, send_im[:, low:]))
+    part_b = lax.all_to_all(send_b, "sky", split_axis=0, concat_axis=0, tiled=True)
+    var_share, part_b = lax.optimization_barrier((var_share, part_b))
+
+    def ranks(values, lower, upper):
+        return values.reshape(n_sky, held_most, -1)[:, lower:upper].reshape(n_sky * (upper - lower), -1)
+
+    image_pos = ()
+    for lower, upper, part in ((0, low, part_a), (low, held_most, part_b)):
+        image_pos = image_field(
+            tuple(ranks(values, lower, upper)[:, 0] for values in where),
+            ranks(weight, lower, upper)[:, 0],
+            ranks(got_coef, lower, upper).reshape(-1),
+            part.reshape(n_sky * (upper - lower), tile, tile),
+            row_side, col_side, extra, (n_visit, GRID * tile + EXTRA, per_dev * tile), image_pos,
+        )
     image_share = reduce_scatter_visit(image_pos, n_visit)
 
     body_rows = GRID * tile

time: 182 us -> 192 us (1.055)
  the two profiles are of different devices: /device:TPU:20 before, /device:TPU:2 now
where the time goes in v1:
time: 192 us; the launch traced here: 191 us
  waiting for transfers between devices  86.5 us (45%)
  Pallas kernels  37.9 us (20%)
  local copies, waits for them, and re-layouts  23.3 us (12%)
  other arithmetic  21.9 us (11%)
  starting transfers between devices  17.4 us (9%)
  matrix products  3.25 us (2%)
    all_to_all x1, waiting for transfers between devices, shards(): lax.all_to_all(send_vm, 'sky', split_axis=0, concat_axis=0, tiled=True)  48.3 us
    pallas_call x2, Pallas kernels, image_field(): pl.pallas_call(image_kernel, out_shape=halves_of(field_shape), in_specs=[...  31 us
    ppermute x4, waiting for transfers between devices, reduce_scatter_visit(): field = keep + lax.ppermute(send, 'visit', perm=pairs)  29.3 us
    all_to_all x1, waiting for transfers between devices, shards(): lax.all_to_all(send_im[:, :low], 'sky', split_axis=0, concat_axis=0, tile...  8.98 us
    pallas_call x1, Pallas kernels, variance_field(): pl.pallas_call(variance_kernel, out_shape=halves_of(field_shape), in_spec...  6.92 us
    all_to_all x1, starting transfers between devices, shards(): lax.all_to_all(send_vm, 'sky', split_axis=0, concat_axis=0, tiled=True)  6.33 us
    all_to_all x1, starting transfers between devices, shards(): lax.all_to_all(send_b, 'sky', split_axis=0, concat_axis=0, tiled=True)  4.72 us
    add x3, other arithmetic, reduce_scatter_visit(): field = keep + lax.ppermute(send, 'visit', perm=pairs)  4.56 us
  transfers between devices with their start and end apart: 7, of which 4 were waited for; matrix products, arithmetic and copies ran while one was open for 15% of the time, Pallas kernels for 11%

profile of v1, /device:TPU:2, one launch (start us, length us, event | category | flops | bytes accessed | tf_op | source)
XLA Modules:
  0.0 191.2 jit_solution(8239327767130323165)
XLA Ops:
  1.3 0.9 convert_reduce_fusion.2
  3.3 0.8 copy.32
  4.1 1.5 maximum_maximum_fusion
  5.8 2.3 %gather_fusion = bf16[64,144,128]{2,1,0:T(8,128)(2,1)} fusion(bf16[33,144,128]{2,1,0:T(8,128)(2,1)S(1)} %concatenate.23, s32[1024]{0:T(1024)S(1)} %pad_clamp_fusion.1), kind=kCustom, calls=%fused_computation | custom fusion | bytes 4718848 | tf_op jit(solution)/shard_map/jit(_take)/gather | solution.py:195
  8.0 6.3 %all-to-all-start = ((bf16[8,8,144,128]{3,2,1,0:T(8,128)(2,1)}), bf16[8,8,144,128]{3,2,1,0:T(8,128)(2,1)S(1)}, u32[]{:S(2)}, u32[]{:S(2)}) async-start(bf16[8,8,144,128]{3,2,1,0:T(8,128)(2,1)} %bitcast.80), calls=%async_computation | async-start | bytes 4718592 | tf_op jit(solution)/shard_map/all_to_all | solution.py:202
  14.4 1.3 concatenate.24
  15.7 2.2 %gather_fusion.1 = bf16[64,128,128]{2,1,0:T(8,128)(2,1)} fusion(bf16[33,128,128]{2,1,0:T(8,128)(2,1)S(1)} %concatenate.24, s32[1024]{0:T(1024)S(1)} %pad_clamp_fusion.1), kind=kCustom, calls=%fused_computation.1 | custom fusion | bytes 4194560 | tf_op jit(solution)/shard_map/jit(_take)/gather | solution.py:195
  17.9 1.5 fusion.6
  19.4 48.3 %all-to-all-done = bf16[8,8,144,128]{3,2,1,0:T(8,128)(2,1)S(1)} async-done(((bf16[8,8,144,128]{3,2,1,0:T(8,128)(2,1)}), bf16[8,8,144,128]{3,2,1,0:T(8,128)(2,1)S(1)}, u32[]{:S(2)}, u32[]{:S(2)}) %all-to-all-start) | async-done | bytes 2359328 | tf_op jit(solution)/shard_map/all_to_all | solution.py:202
  70.2 1.5 fusion.40
  71.6 4.2 %all-to-all-start.1 = ((bf16[8,4,128,128]{3,2,1,0:T(8,128)(2,1)}), bf16[8,4,128,128]{3,2,1,0:T(8,128)(2,1)S(1)}, u32[]{:S(2)}, u32[]{:S(2)}) async-start(bf16[8,4,128,128]{3,2,1,0:T(8,128)(2,1)} %get-tuple-element.50), calls=%async_computation.1 | async-start | bytes 2097152 | tf_op jit(solution)/shard_map/all_to_all | solution.py:243
  76.4 6.9 %shard_map.94 = (f32[2,1024,256]{2,1,0:T(8,128)}, f32[2,1024,256]{2,1,0:T(8,128)}) custom-call(s32[64]{0:T(128)} %get-tuple-element.71.row_ref, s32[64]{0:T(128)} %get-tuple-element.70.group_ref, s32[64]{0:T(128)} %get-tuple-element.46.sub_ref, f32[64]{0:T(128)} %mul.54.w2_ref, bf16[64,144,128]{2,1,0:T(8,128)(2,1)} %bitcast.79), custom_call_target="tpu_custom_call" | custom-call | tf_op jit(solution)/shard_map/pallas_call | solution.py:114
  83.4 1.5 fusion.7
  84.8 1.1 copy.36
  86.0 0.9 copy.42.col_side_ref
  86.9 1.3 copy.35
  88.2 0.9 copy.41.row_side_ref
  92.2 9.0 %all-to-all-done.1 = bf16[8,4,128,128]{3,2,1,0:T(8,128)(2,1)S(1)} async-done(((bf16[8,4,128,128]{3,2,1,0:T(8,128)(2,1)}), bf16[8,4,128,128]{3,2,1,0:T(8,128)(2,1)S(1)}, u32[]{:S(2)}, u32[]{:S(2)}) %all-to-all-start.1) | async-done | bytes 1048608 | tf_op jit(solution)/shard_map/all_to_all | solution.py:243
  101.2 4.7 %all-to-all-start.2 = ((bf16[8,4,128,128]{3,2,1,0:T(8,128)(2,1)}), bf16[8,4,128,128]{3,2,1,0:T(8,128)(2,1)}, u32[]{:S(2)}, u32[]{:S(2)}) async-start(bf16[8,4,128,128]{3,2,1,0:T(8,128)(2,1)} %get-tuple-element.22), calls=%async_computation.2 | async-start | bytes 2097152 | tf_op jit(solution)/shard_map/all_to_all | solution.py:245
  106.0 1.3 copy-done.3
  107.4 2.5 %add.164 = f32[2,1024,256]{2,1,0:T(8,128)S(1)} add(f32[2,1024,256]{2,1,0:T(8,128)} %get-tuple-element.19, f32[2,1024,256]{2,1,0:T(8,128)} %copy-done.3) | non-fusion elementwise | flops 524288 | bytes 6291456 | tf_op jit(solution)/shard_map/add | solution.py:152
  109.9 1.0 slice.117
  110.9 1.5 collective-permute-start.1
  117.8 1.6 sort.31
  119.5 1.6 sort.32
  122.4 14.8 %shard_map.95 = (f32[2,1032,256]{2,1,0:T(8,128)}, f32[2,1032,256]{2,1,0:T(8,128)}) custom-call(s32[32]{0:T(128)} %get-tuple-element.24.order_ref, s32[1]{0:T(128)} %bitcast.25.count_ref, s32[32]{0:T(128)} %copy-done.6, s32[32]{0:T(128)} %squeeze_reshape.29.group_ref, s32[32]{0:T(128)} %squeeze_reshape.30.sub_ref, f32[32]{0:T(128)} %squeeze_reshape.31.w_ref, ...), custom_call_target="tpu_custom_call" | custom-call | flops 2415919104 | bytes 5275648 | tf_op jit(solution)/shard_map/pallas_call | solution.py:126
  137.3 1.4 fusion.9
  138.7 16.2 %shard_map.96 = (f32[2,1032,256]{2,1,0:T(8,128)}, f32[2,1032,256]{2,1,0:T(8,128)}) custom-call(s32[32]{0:T(128)} %get-tuple-element.18.order_ref, s32[1]{0:T(128)} %bitcast.10.count_ref, s32[32]{0:T(128)} %copy-done.5, s32[32]{0:T(128)} %squeeze_reshape.25.group_ref, s32[32]{0:T(128)} %squeeze_reshape.26.sub_ref, ...), custom_call_target="tpu_custom_call", output_to_operand_aliasing={{0}: (11, {}), {1}: (12, {})} | custom-call | flops 2415919104 | bytes 5275648 | tf_op jit(solution)/shard_map/pallas_call | solution.py:126
  154.9 4.4 %collective-permute-done.2 = f32[2,1032,256]{2,1,0:T(8,128)S(1)} collective-permute-done((f32[2,1032,256]{2,1,0:T(8,128)}, f32[2,1032,256]{2,1,0:T(8,128)S(1)}, u32[]{:S(2)}, u32[]{:S(2)}) %collective-permute-start.2) | collective-permute-done | bytes 2113568 | tf_op jit(solution)/shard_map/ppermute | solution.py:152
  159.3 1.9 %add.169 = f32[2,1032,256]{2,1,0:T(8,128)S(1)} add(f32[2,1032,256]{2,1,0:T(8,128)} %get-tuple-element.28, f32[2,1032,256]{2,1,0:T(8,128)S(1)} %collective-permute-done.2) | non-fusion elementwise | flops 528384 | bytes 6340608 | tf_op jit(solution)/shard_map/add | solution.py:152
  161.9 24.9 %collective-permute-done.3 = f32[1,1032,256]{2,1,0:T(8,128)S(1)} collective-permute-done((f32[1,1032,256]{2,1,0:T(8,128)S(1)}, f32[1,1032,256]{2,1,0:T(8,128)S(1)}, u32[]{:S(2)}, u32[]{:S(2)}) %collective-permute-start.3) | collective-permute-done | bytes 1056800 | tf_op jit(solution)/shard_map/ppermute | solution.py:152
  189.5 1.7 fusion.8
  (96 shorter events, 18.3 us)
Async XLA Ops:
  0.6 82.7 %copy-start = (bf16[9,41]{1,0:T(8,128)(2,1)S(1)}, bf16[9,41]{1,0:T(8,128)(2,1)}, u32[]{:S(2)}) copy-start(bf16[9,41]{1,0:T(8,128)(2,1)} %param.12) | copy-start | bytes 2218
  8.0 59.6 %all-to-all-start = ((bf16[8,8,144,128]{3,2,1,0:T(8,128)(2,1)}), bf16[8,8,144,128]{3,2,1,0:T(8,128)(2,1)S(1)}, u32[]{:S(2)}, u32[]{:S(2)}) async-start(bf16[8,8,144,128]{3,2,1,0:T(8,128)(2,1)} %bitcast.80), calls=%async_computation | async-start | bytes 4718592 | tf_op jit(solution)/shard_map/all_to_all | solution.py:202
  15.7 2.2 %copy-start.8 = (bf16[9,41]{1,0:T(8,128)(2,1)S(1)}, bf16[9,41]{1,0:T(8,128)(2,1)}, u32[]{:S(2)}) copy-start(bf16[9,41]{1,0:T(8,128)(2,1)} %param.13) | copy-start | bytes 2218
  67.7 4.0 %copy-start.1 = (bf16[8,8,144,128]{3,2,1,0:T(8,128)(2,1)}, bf16[8,8,144,128]{3,2,1,0:T(8,128)(2,1)S(1)}, u32[]{:S(2)}) copy-start(bf16[8,8,144,128]{3,2,1,0:T(8,128)(2,1)S(1)} %all-to-all-done) | copy-start | bytes 7077892
  67.7 2.5 %copy-start.2 = (bf16[64,128,128]{2,1,0:T(8,128)(2,1)S(1)}, bf16[64,128,128]{2,1,0:T(8,128)(2,1)}, u32[]{:S(2)}) copy-start(bf16[64,128,128]{2,1,0:T(8,128)(2,1)} %gather_fusion.1) | copy-start | bytes 6291460
  69.6 2.1 %copy-start.7 = (f32[64]{0:T(128)}, f32[64]{0:T(128)S(1)}, u32[]{:S(2)}) copy-start(f32[64]{0:T(128)S(1)} %get-tuple-element.45) | copy-start | bytes 772
  71.6 29.5 %all-to-all-start.1 = ((bf16[8,4,128,128]{3,2,1,0:T(8,128)(2,1)}), bf16[8,4,128,128]{3,2,1,0:T(8,128)(2,1)S(1)}, u32[]{:S(2)}, u32[]{:S(2)}) async-start(bf16[8,4,128,128]{3,2,1,0:T(8,128)(2,1)} %get-tuple-element.50), calls=%async_computation.1 | async-start | bytes 2097152 | tf_op jit(solution)/shard_map/all_to_all | solution.py:243
  83.4 22.7 %collective-permute-start = (f32[2,1024,256]{2,1,0:T(8,128)}, f32[2,1024,256]{2,1,0:T(8,128)S(1)}, u32[]{:S(2)}, u32[]{:S(2)}) collective-permute-start(f32[2,1024,256]{2,1,0:T(8,128)} %get-tuple-element.20), channel_id=1, source_target_pairs={{0,1},{1,0},{2,3},{3,2},{4,5},{5,4},{6,7},{7,6},{8,9},{9,8},{10,11... | collective-permute-start | bytes 6291464 | tf_op jit(solution)/shard_map/ppermute | solution.py:152
  101.2 8.7 %copy-start.4 = (bf16[8,4,128,128]{3,2,1,0:T(8,128)(2,1)}, bf16[8,4,128,128]{3,2,1,0:T(8,128)(2,1)S(1)}, u32[]{:S(2)}) copy-start(bf16[8,4,128,128]{3,2,1,0:T(8,128)(2,1)S(1)} %all-to-all-done.1) | copy-start | bytes 3145732
  101.2 37.5 %all-to-all-start.2 = ((bf16[8,4,128,128]{3,2,1,0:T(8,128)(2,1)}), bf16[8,4,128,128]{3,2,1,0:T(8,128)(2,1)}, u32[]{:S(2)}, u32[]{:S(2)}) async-start(bf16[8,4,128,128]{3,2,1,0:T(8,128)(2,1)} %get-tuple-element.22), calls=%async_computation.2 | async-start | bytes 2097152 | tf_op jit(solution)/shard_map/all_to_all | solution.py:245
  106.0 1.3 copy-start.3
  110.9 26.3 %collective-permute-start.1 = (f32[1,1024,256]{2,1,0:T(8,128)}, f32[1,1024,256]{2,1,0:T(8,128)}, u32[]{:S(2)}, u32[]{:S(2)}) collective-permute-start(f32[1,1024,256]{2,1,0:T(8,128)} %slice.117), channel_id=1, source_target_pairs={{0,2},{1,3},{2,0},{3,1},{4,6},{5,7},{6,4},{7,5},{8,10},{9,11},{10,... | collective-permute-start | bytes 3145736 | tf_op jit(solution)/shard_map/ppermute | solution.py:152
  115.1 7.4 %copy-start.6 = (s32[32]{0:T(128)}, s32[32]{0:T(128)S(1)}, u32[]{:S(2)}) copy-start(s32[32]{0:T(128)S(1)} %squeeze_reshape.28.row_ref) | copy-start | bytes 388
  115.2 22.1 %copy-start.5 = (s32[32]{0:T(128)}, s32[32]{0:T(128)S(1)}, u32[]{:S(2)}) copy-start(s32[32]{0:T(128)S(1)} %squeeze_reshape.24.row_ref) | copy-start | bytes 388
  154.9 4.4 %collective-permute-start.2 = (f32[2,1032,256]{2,1,0:T(8,128)}, f32[2,1032,256]{2,1,0:T(8,128)S(1)}, u32[]{:S(2)}, u32[]{:S(2)}) collective-permute-start(f32[2,1032,256]{2,1,0:T(8,128)} %get-tuple-element.29), channel_id=1, source_target_pairs={{0,1},{1,0},{2,3},{3,2},{4,5},{5,4},{6,7},{7,6},{8,9},{9,8},{10,11... | collective-permute-start | bytes 6340616 | tf_op jit(solution)/shard_map/ppermute | solution.py:152
  161.3 26.9 %copy-start.9 = (bf16[9,41]{1,0:T(8,128)(2,1)S(1)}, bf16[9,41]{1,0:T(8,128)(2,1)}, u32[]{:S(2)}) copy-start(bf16[9,41]{1,0:T(8,128)(2,1)} %param.13) | copy-start | bytes 2218
  161.3 25.4 %collective-permute-start.3 = (f32[1,1032,256]{2,1,0:T(8,128)S(1)}, f32[1,1032,256]{2,1,0:T(8,128)S(1)}, u32[]{:S(2)}, u32[]{:S(2)}) collective-permute-start(f32[1,1032,256]{2,1,0:T(8,128)S(1)} %slice.120), channel_id=1, source_target_pairs={{0,2},{1,3},{2,0},{3,1},{4,6},{5,7},{6,4},{7,5},{8,10},{9,11},{10,... | collective-permute-start | bytes 3170312 | tf_op jit(solution)/shard_map/ppermute | solution.py:152

commit v2 on v0

--- a/solution.py
+++ b/solution.py
@@ -77,8 +77,12 @@
                 for h in range(2)
             ]
             blocks.append(jnp.concatenate(halves, axis=1))
-        scaled = jnp.concatenate(blocks, axis=0)
-        matched = jnp.dot(col_side_ref[...], scaled, preferred_element_type=jnp.float32)
+        matched = jnp.dot(col_side_ref[:, :tile], blocks[0], preferred_element_type=jnp.float32)
+        for k in range(1, BASIS):
+            matched = matched + jnp.dot(
+                col_side_ref[:, k * tile:(k + 1) * tile], blocks[k],
+                preferred_element_type=jnp.float32,
+            )
         for h in range(2):
             t = pair[h]
             row = row_ref[t]

time: 182 us -> 185 us (1.016)
  the two profiles are of different devices: /device:TPU:20 before, /device:TPU:0 now
where the time goes in v2:
time: 185 us; the launch traced here: 187 us
  waiting for transfers between devices  102 us (55%)
  Pallas kernels  33.5 us (18%)
  other arithmetic  20 us (11%)
  starting transfers between devices  14.8 us (8%)
  local copies, waits for them, and re-layouts  14 us (8%)
    all_to_all x1, waiting for transfers between devices, shards(): lax.all_to_all(send_vm, 'sky', split_axis=0, concat_axis=0, tiled=True)  50.4 us
    ppermute x4, waiting for transfers between devices, reduce_scatter_visit(): field = keep + lax.ppermute(send, 'visit', perm=pairs)  47.9 us
    pallas_call x1, Pallas kernels, image_field(): pl.pallas_call(image_kernel, out_shape=halves_of(field_shape), in_specs=[...  26.5 us
    all_to_all x1, starting transfers between devices, shards(): lax.all_to_all(send_vm, 'sky', split_axis=0, concat_axis=0, tiled=True)  7.25 us
    pallas_call x1, Pallas kernels, variance_field(): pl.pallas_call(variance_kernel, out_shape=halves_of(field_shape), in_spec...  7 us
    add x3, other arithmetic, reduce_scatter_visit(): field = keep + lax.ppermute(send, 'visit', perm=pairs)  4.56 us
    gather x2, local copies, waits for them, and re-layouts, gather_slots(): jnp.take(padded, source_tile, axis=0, mode='clip')  4.4 us
    all_to_all x1, starting transfers between devices, shards(): lax.all_to_all(send_im, 'sky', split_axis=0, concat_axis=0, tiled=True)  4.35 us
  transfers between devices with their start and end apart: 6, of which 5 were waited for; matrix products, arithmetic and copies ran while one was open for 10% of the time, Pallas kernels for 4%

profile of v2, /device:TPU:0, one launch (start us, length us, event | category | flops | bytes accessed | tf_op | source)
XLA Modules:
  0.0 186.6 jit_solution(1686534335706869711)
XLA Ops:
  0.6 0.9 convert_reduce_fusion.2
  1.6 0.7 multiply_add_fusion.1
  3.1 0.8 copy.28
  4.2 1.5 maximum_maximum_fusion
  5.8 2.3 %gather_fusion = bf16[64,144,128]{2,1,0:T(8,128)(2,1)} fusion(bf16[33,144,128]{2,1,0:T(8,128)(2,1)S(1)} %concatenate.23, s32[1024]{0:T(1024)S(1)} %pad_clamp_fusion.1), kind=kCustom, calls=%fused_computation | custom fusion | bytes 4718848 | tf_op jit(solution)/shard_map/jit(_take)/gather | solution.py:194
  8.0 7.3 %all-to-all-start = ((bf16[8,8,144,128]{3,2,1,0:T(8,128)(2,1)}), bf16[8,8,144,128]{3,2,1,0:T(8,128)(2,1)S(1)}, u32[]{:S(2)}, u32[]{:S(2)}) async-start(bf16[8,8,144,128]{3,2,1,0:T(8,128)(2,1)} %bitcast.60), calls=%async_computation | async-start | bytes 4718592 | tf_op jit(solution)/shard_map/all_to_all | solution.py:201
  15.3 1.3 concatenate.24
  16.6 2.1 %gather_fusion.1 = bf16[64,128,128]{2,1,0:T(8,128)(2,1)} fusion(bf16[33,128,128]{2,1,0:T(8,128)(2,1)S(1)} %concatenate.24, s32[1024]{0:T(1024)S(1)} %pad_clamp_fusion.1), kind=kCustom, calls=%fused_computation.1 | custom fusion | bytes 4194560 | tf_op jit(solution)/shard_map/jit(_take)/gather | solution.py:194
  18.7 50.4 %all-to-all-done = bf16[8,8,144,128]{3,2,1,0:T(8,128)(2,1)S(1)} async-done(((bf16[8,8,144,128]{3,2,1,0:T(8,128)(2,1)}), bf16[8,8,144,128]{3,2,1,0:T(8,128)(2,1)S(1)}, u32[]{:S(2)}, u32[]{:S(2)}) %all-to-all-start) | async-done | bytes 2359328 | tf_op jit(solution)/shard_map/all_to_all | solution.py:201
  71.6 4.3 %all-to-all-start.1 = ((bf16[8,8,128,128]{3,2,1,0:T(8,128)(2,1)}), bf16[8,8,128,128]{3,2,1,0:T(8,128)(2,1)}, u32[]{:S(2)}, u32[]{:S(2)}) async-start(bf16[8,8,128,128]{3,2,1,0:T(8,128)(2,1)} %bitcast.61), calls=%async_computation.1 | async-start | bytes 4194304 | tf_op jit(solution)/shard_map/all_to_all | solution.py:241
  76.0 1.3 fusion.31
  77.3 7.0 %shard_map.94 = (f32[2,1024,256]{2,1,0:T(8,128)}, f32[2,1024,256]{2,1,0:T(8,128)}) custom-call(s32[64]{0:T(128)} %get-tuple-element.38.row_ref, s32[64]{0:T(128)} %get-tuple-element.44.group_ref, s32[64]{0:T(128)} %get-tuple-element.34.sub_ref, f32[64]{0:T(128)} %mul.54.w2_ref, bf16[64,144,128]{2,1,0:T(8,128)(2,1)} %bitcast.59), custom_call_target="tpu_custom_call" | custom-call | tf_op jit(solution)/shard_map/pallas_call | solution.py:114
  84.3 0.7 fusion.7
  85.4 0.9 copy.35.row_side_ref
  86.3 0.7 fusion.6
  87.0 0.9 copy.36.col_side_ref
  89.1 1.3 copy-done.2
  90.4 2.5 %add.106 = f32[2,1024,256]{2,1,0:T(8,128)S(1)} add(f32[2,1024,256]{2,1,0:T(8,128)} %get-tuple-element.14, f32[2,1024,256]{2,1,0:T(8,128)} %copy-done.2) | non-fusion elementwise | flops 524288 | bytes 6291456 | tf_op jit(solution)/shard_map/add | solution.py:151
  93.0 1.6 collective-permute-start.1
  95.0 0.7 reshape.184.coef_ref
  95.7 2.1 %sort.17 = (pred[64]{0:T(512)(128)(4,1)}, s32[64]{0:T(128)}) sort(pred[64]{0:T(512)(128)(4,1)S(1)} %compare_not_fusion, s32[64]{0:T(128)S(1)} %iota.46), dimensions={0}, to_apply=%region_3.4 | sort | flops 384 | bytes 640 | tf_op jit(solution)/shard_map/jit(argsort)/sort | solution.py:124
  97.8 0.7 pad_maximum_fusion
  98.5 0.7 maximum_maximum_fusion.1.extra_ref
  99.2 19.6 %collective-permute-done.1 = f32[1,1024,256]{2,1,0:T(8,128)} collective-permute-done((f32[1,1024,256]{2,1,0:T(8,128)S(1)}, f32[1,1024,256]{2,1,0:T(8,128)}, u32[]{:S(2)}, u32[]{:S(2)}) %collective-permute-start.1) | collective-permute-done | bytes 1048608 | tf_op jit(solution)/shard_map/ppermute | solution.py:151
  118.8 1.4 fusion.9
  120.2 3.6 %all-to-all-done.1 = bf16[8,8,128,128]{3,2,1,0:T(8,128)(2,1)} async-done(((bf16[8,8,128,128]{3,2,1,0:T(8,128)(2,1)}), bf16[8,8,128,128]{3,2,1,0:T(8,128)(2,1)}, u32[]{:S(2)}, u32[]{:S(2)}) %all-to-all-start.1) | async-done | bytes 2097184 | tf_op jit(solution)/shard_map/all_to_all | solution.py:241
  123.8 26.5 %shard_map.95 = (f32[2,1032,256]{2,1,0:T(8,128)}, f32[2,1032,256]{2,1,0:T(8,128)}) custom-call(s32[64]{0:T(128)} %get-tuple-element.13.order_ref, s32[1]{0:T(128)} %bitcast.10.count_ref, s32[64]{0:T(128)} %get-tuple-element.38.row_ref, s32[64]{0:T(128)} %get-tuple-element.44.group_ref, s32[64]{0:T(128)} %get-tuple-element.34.sub_ref, f32[64]{0:T(128)} %copy-done.4, ...), custom_call_target="tpu_custom_call" | custom-call | flops 4831838208 | bytes 6324224 | tf_op jit(solution)/shard_map/pallas_call | solution.py:126
  150.3 4.4 %collective-permute-done.2 = f32[2,1032,256]{2,1,0:T(8,128)S(1)} collective-permute-done((f32[2,1032,256]{2,1,0:T(8,128)}, f32[2,1032,256]{2,1,0:T(8,128)S(1)}, u32[]{:S(2)}, u32[]{:S(2)}) %collective-permute-start.2) | collective-permute-done | bytes 2113568 | tf_op jit(solution)/shard_map/ppermute | solution.py:151
  154.7 1.9 %add.111 = f32[2,1032,256]{2,1,0:T(8,128)S(1)} add(f32[2,1032,256]{2,1,0:T(8,128)} %get-tuple-element.18, f32[2,1032,256]{2,1,0:T(8,128)S(1)} %collective-permute-done.2) | non-fusion elementwise | flops 528384 | bytes 6340608 | tf_op jit(solution)/shard_map/add | solution.py:151
  156.7 1.6 collective-permute-start.3
  158.3 23.9 %collective-permute-done.3 = f32[1,1032,256]{2,1,0:T(8,128)S(1)} collective-permute-done((f32[1,1032,256]{2,1,0:T(8,128)S(1)}, f32[1,1032,256]{2,1,0:T(8,128)S(1)}, u32[]{:S(2)}, u32[]{:S(2)}) %collective-permute-start.3) | collective-permute-done | bytes 1056800 | tf_op jit(solution)/shard_map/ppermute | solution.py:151
  184.9 1.7 fusion.8
  (64 shorter events, 8.5 us)
Async XLA Ops:
  0.6 83.7 %copy-start = (bf16[9,41]{1,0:T(8,128)(2,1)S(1)}, bf16[9,41]{1,0:T(8,128)(2,1)}, u32[]{:S(2)}) copy-start(bf16[9,41]{1,0:T(8,128)(2,1)} %param.12) | copy-start | bytes 2218
  8.0 61.1 %all-to-all-start = ((bf16[8,8,144,128]{3,2,1,0:T(8,128)(2,1)}), bf16[8,8,144,128]{3,2,1,0:T(8,128)(2,1)S(1)}, u32[]{:S(2)}, u32[]{:S(2)}) async-start(bf16[8,8,144,128]{3,2,1,0:T(8,128)(2,1)} %bitcast.60), calls=%async_computation | async-start | bytes 4718592 | tf_op jit(solution)/shard_map/all_to_all | solution.py:201
  69.1 2.5 %copy-start.1 = (bf16[8,8,144,128]{3,2,1,0:T(8,128)(2,1)}, bf16[8,8,144,128]{3,2,1,0:T(8,128)(2,1)S(1)}, u32[]{:S(2)}) copy-start(bf16[8,8,144,128]{3,2,1,0:T(8,128)(2,1)S(1)} %all-to-all-done) | copy-start | bytes 7077892
  71.1 17.0 %copy-start.4 = (f32[64]{0:T(128)}, f32[64]{0:T(128)S(1)}, u32[]{:S(2)}) copy-start(f32[64]{0:T(128)S(1)} %get-tuple-element.33.w_ref) | copy-start | bytes 772
  71.6 52.2 %all-to-all-start.1 = ((bf16[8,8,128,128]{3,2,1,0:T(8,128)(2,1)}), bf16[8,8,128,128]{3,2,1,0:T(8,128)(2,1)}, u32[]{:S(2)}, u32[]{:S(2)}) async-start(bf16[8,8,128,128]{3,2,1,0:T(8,128)(2,1)} %bitcast.61), calls=%async_computation.1 | async-start | bytes 4194304 | tf_op jit(solution)/shard_map/all_to_all | solution.py:241
  77.3 9.0 %copy-start.5 = (bf16[9,41]{1,0:T(8,128)(2,1)S(1)}, bf16[9,41]{1,0:T(8,128)(2,1)}, u32[]{:S(2)}) copy-start(bf16[9,41]{1,0:T(8,128)(2,1)} %param.13) | copy-start | bytes 2218
  84.3 4.8 %collective-permute-start = (f32[2,1024,256]{2,1,0:T(8,128)}, f32[2,1024,256]{2,1,0:T(8,128)S(1)}, u32[]{:S(2)}, u32[]{:S(2)}) collective-permute-start(f32[2,1024,256]{2,1,0:T(8,128)} %get-tuple-element.15), channel_id=1, source_target_pairs={{0,1},{1,0},{2,3},{3,2},{4,5},{5,4},{6,7},{7,6},{8,9},{9,8},{10,11... | collective-permute-start | bytes 6291464 | tf_op jit(solution)/shard_map/ppermute | solution.py:151
  89.1 1.4 copy-start.2
  92.9 2.8 %copy-start.3 = (s32[64]{0:T(128)S(1)}, s32[64]{0:T(128)}, u32[]{:S(2)}) copy-start(s32[64]{0:T(128)} %get-tuple-element.38.row_ref) | copy-start | bytes 772
  93.0 25.7 %collective-permute-start.1 = (f32[1,1024,256]{2,1,0:T(8,128)S(1)}, f32[1,1024,256]{2,1,0:T(8,128)}, u32[]{:S(2)}, u32[]{:S(2)}) collective-permute-start(f32[1,1024,256]{2,1,0:T(8,128)S(1)} %slice.68), channel_id=1, source_target_pairs={{0,2},{1,3},{2,0},{3,1},{4,6},{5,7},{6,4},{7,5},{8,10},{9,11},{10,... | collective-permute-start | bytes 3145736 | tf_op jit(solution)/shard_map/ppermute | solution.py:151
  150.3 4.4 %collective-permute-start.2 = (f32[2,1032,256]{2,1,0:T(8,128)}, f32[2,1032,256]{2,1,0:T(8,128)S(1)}, u32[]{:S(2)}, u32[]{:S(2)}) collective-permute-start(f32[2,1032,256]{2,1,0:T(8,128)} %get-tuple-element.19), channel_id=1, source_target_pairs={{0,1},{1,0},{2,3},{3,2},{4,5},{5,4},{6,7},{7,6},{8,9},{9,8},{10,11... | collective-permute-start | bytes 6340616 | tf_op jit(solution)/shard_map/ppermute | solution.py:151
  156.7 25.4 %collective-permute-start.3 = (f32[1,1032,256]{2,1,0:T(8,128)S(1)}, f32[1,1032,256]{2,1,0:T(8,128)S(1)}, u32[]{:S(2)}, u32[]{:S(2)}) collective-permute-start(f32[1,1032,256]{2,1,0:T(8,128)S(1)} %slice.70), channel_id=1, source_target_pairs={{0,2},{1,3},{2,0},{3,1},{4,6},{5,7},{6,4},{7,5},{8,10},{9,11},{10,... | collective-permute-start | bytes 3170312 | tf_op jit(solution)/shard_map/ppermute | solution.py:151

commit v3 on v0

--- a/solution.py
+++ b/solution.py
@@ -9,6 +9,7 @@
 BASIS = 9
 META = 16
 EXTRA = 8
+GANG = 4
 
 
 weight_floor = 0.5
@@ -66,20 +67,20 @@
         out_ref[:, body_rows:, :] = extra_ref[which * half:(which + 1) * half]
 
     def body(p, carry):
-        pair = (order_ref[2 * p], order_ref[2 * p + 1])
-        both = jnp.concatenate([img_ref[pair[0]], img_ref[pair[1]]], axis=0)
+        pair = tuple(order_ref[GANG * p + h] for h in range(GANG))
+        both = jnp.concatenate([img_ref[t] for t in pair], axis=0)
         first = jnp.dot(both, row_side_ref[...], preferred_element_type=jnp.float32)
         blocks = []
         for k in range(BASIS):
             halves = [
                 (first[h * tile:(h + 1) * tile, k * tile:(k + 1) * tile]
                  * coef_ref[pair[h] * BASIS + k]).astype(jnp.bfloat16)
-                for h in range(2)
+                for h in range(GANG)
             ]
             blocks.append(jnp.concatenate(halves, axis=1))
         scaled = jnp.concatenate(blocks, axis=0)
         matched = jnp.dot(col_side_ref[...], scaled, preferred_element_type=jnp.float32)
-        for h in range(2):
+        for h in range(GANG):
             t = pair[h]
             row = row_ref[t]
 
@@ -90,7 +91,7 @@
 
         return carry
 
-    lax.fori_loop(0, (count_ref[0] + 1) // 2, body, 0)
+    lax.fori_loop(0, (count_ref[0] + GANG - 1) // GANG, body, 0)
 
 
 def smem():

time: 182 us -> 175 us (0.962)
  the two profiles are of different devices: /device:TPU:20 before, /device:TPU:6 now
where the time goes in v3:
time: 175 us; the launch traced here: 176 us
  waiting for transfers between devices  103 us (59%)
  Pallas kernels  24.5 us (14%)
  other arithmetic  20 us (11%)
  local copies, waits for them, and re-layouts  14 us (8%)
  starting transfers between devices  12.3 us (7%)
    all_to_all x1, waiting for transfers between devices, shards(): lax.all_to_all(send_vm, 'sky', split_axis=0, concat_axis=0, tiled=True)  49.8 us
    ppermute x4, waiting for transfers between devices, reduce_scatter_visit(): field = keep + lax.ppermute(send, 'visit', perm=pairs)  49.8 us
    pallas_call x1, Pallas kernels, image_field(): pl.pallas_call(image_kernel, out_shape=halves_of(field_shape), in_specs=[...  17.5 us
    pallas_call x1, Pallas kernels, variance_field(): pl.pallas_call(variance_kernel, out_shape=halves_of(field_shape), in_spec...  6.99 us
    all_to_all x1, starting transfers between devices, shards(): lax.all_to_all(send_vm, 'sky', split_axis=0, concat_axis=0, tiled=True)  6.34 us
    all_to_all x1, starting transfers between devices, shards(): lax.all_to_all(send_im, 'sky', split_axis=0, concat_axis=0, tiled=True)  4.78 us
    add x3, other arithmetic, reduce_scatter_visit(): field = keep + lax.ppermute(send, 'visit', perm=pairs)  4.56 us
    gather x2, local copies, waits for them, and re-layouts, gather_slots(): jnp.take(padded, source_tile, axis=0, mode='clip')  4.4 us
  transfers between devices with their start and end apart: 6, of which 5 were waited for; matrix products, arithmetic and copies ran while one was open for 10% of the time, Pallas kernels for 4%

profile of v3, /device:TPU:6, one launch (start us, length us, event | category | flops | bytes accessed | tf_op | source)
XLA Modules:
  0.0 176.2 jit_solution(5708163324335623056)
XLA Ops:
  0.6 0.9 convert_reduce_fusion.2
  1.6 0.7 multiply_add_fusion.1
  2.3 0.7 convert_bitcast_fusion
  3.1 0.8 copy.28
  4.2 1.5 maximum_maximum_fusion
  5.8 2.3 %gather_fusion = bf16[64,144,128]{2,1,0:T(8,128)(2,1)} fusion(bf16[33,144,128]{2,1,0:T(8,128)(2,1)S(1)} %concatenate.23, s32[1024]{0:T(1024)S(1)} %pad_clamp_fusion.1), kind=kCustom, calls=%fused_computation | custom fusion | bytes 4718848 | tf_op jit(solution)/shard_map/jit(_take)/gather | solution.py:191
  8.0 6.3 %all-to-all-start = ((bf16[8,8,144,128]{3,2,1,0:T(8,128)(2,1)}), bf16[8,8,144,128]{3,2,1,0:T(8,128)(2,1)S(1)}, u32[]{:S(2)}, u32[]{:S(2)}) async-start(bf16[8,8,144,128]{3,2,1,0:T(8,128)(2,1)} %bitcast.60), calls=%async_computation | async-start | bytes 4718592 | tf_op jit(solution)/shard_map/all_to_all | solution.py:198
  14.4 1.3 concatenate.24
  15.7 2.1 %gather_fusion.1 = bf16[64,128,128]{2,1,0:T(8,128)(2,1)} fusion(bf16[33,128,128]{2,1,0:T(8,128)(2,1)S(1)} %concatenate.24, s32[1024]{0:T(1024)S(1)} %pad_clamp_fusion.1), kind=kCustom, calls=%fused_computation.1 | custom fusion | bytes 4194560 | tf_op jit(solution)/shard_map/jit(_take)/gather | solution.py:191
  17.8 49.8 %all-to-all-done = bf16[8,8,144,128]{3,2,1,0:T(8,128)(2,1)S(1)} async-done(((bf16[8,8,144,128]{3,2,1,0:T(8,128)(2,1)}), bf16[8,8,144,128]{3,2,1,0:T(8,128)(2,1)S(1)}, u32[]{:S(2)}, u32[]{:S(2)}) %all-to-all-start) | async-done | bytes 2359328 | tf_op jit(solution)/shard_map/all_to_all | solution.py:198
  70.2 4.8 %all-to-all-start.1 = ((bf16[8,8,128,128]{3,2,1,0:T(8,128)(2,1)}), bf16[8,8,128,128]{3,2,1,0:T(8,128)(2,1)}, u32[]{:S(2)}, u32[]{:S(2)}) async-start(bf16[8,8,128,128]{3,2,1,0:T(8,128)(2,1)} %bitcast.61), calls=%async_computation.1 | async-start | bytes 4194304 | tf_op jit(solution)/shard_map/all_to_all | solution.py:238
  74.9 1.3 fusion.31
  76.2 7.0 %shard_map.94 = (f32[2,1024,256]{2,1,0:T(8,128)}, f32[2,1024,256]{2,1,0:T(8,128)}) custom-call(s32[64]{0:T(128)} %get-tuple-element.38.row_ref, s32[64]{0:T(128)} %get-tuple-element.44.group_ref, s32[64]{0:T(128)} %get-tuple-element.34.sub_ref, f32[64]{0:T(128)} %mul.54.w2_ref, bf16[64,144,128]{2,1,0:T(8,128)(2,1)} %bitcast.59), custom_call_target="tpu_custom_call" | custom-call | tf_op jit(solution)/shard_map/pallas_call | solution.py:111
  83.2 0.7 fusion.7
  84.3 0.9 copy.35.row_side_ref
  85.2 0.7 fusion.6
  86.0 0.9 copy.36.col_side_ref
  88.0 1.3 copy-done.2
  89.4 2.5 %add.106 = f32[2,1024,256]{2,1,0:T(8,128)S(1)} add(f32[2,1024,256]{2,1,0:T(8,128)} %get-tuple-element.14, f32[2,1024,256]{2,1,0:T(8,128)} %copy-done.2) | non-fusion elementwise | flops 524288 | bytes 6291456 | tf_op jit(solution)/shard_map/add | solution.py:148
  92.9 0.7 reshape.184.coef_ref
  93.7 2.1 %sort.17 = (pred[64]{0:T(512)(128)(4,1)}, s32[64]{0:T(128)}) sort(pred[64]{0:T(512)(128)(4,1)S(1)} %compare_not_fusion, s32[64]{0:T(128)S(1)} %iota.46), dimensions={0}, to_apply=%region_3.4 | sort | flops 384 | bytes 640 | tf_op jit(solution)/shard_map/jit(argsort)/sort | solution.py:121
  95.7 0.7 pad_maximum_fusion
  96.4 0.7 maximum_maximum_fusion.1.extra_ref
  97.1 20.6 %collective-permute-done.1 = f32[1,1024,256]{2,1,0:T(8,128)} collective-permute-done((f32[1,1024,256]{2,1,0:T(8,128)S(1)}, f32[1,1024,256]{2,1,0:T(8,128)}, u32[]{:S(2)}, u32[]{:S(2)}) %collective-permute-start.1) | collective-permute-done | bytes 1048608 | tf_op jit(solution)/shard_map/ppermute | solution.py:148
  117.7 1.4 fusion.9
  119.1 3.2 %all-to-all-done.1 = bf16[8,8,128,128]{3,2,1,0:T(8,128)(2,1)} async-done(((bf16[8,8,128,128]{3,2,1,0:T(8,128)(2,1)}), bf16[8,8,128,128]{3,2,1,0:T(8,128)(2,1)}, u32[]{:S(2)}, u32[]{:S(2)}) %all-to-all-start.1) | async-done | bytes 2097184 | tf_op jit(solution)/shard_map/all_to_all | solution.py:238
  122.3 17.5 %shard_map.95 = (f32[2,1032,256]{2,1,0:T(8,128)}, f32[2,1032,256]{2,1,0:T(8,128)}) custom-call(s32[64]{0:T(128)} %get-tuple-element.13.order_ref, s32[1]{0:T(128)} %bitcast.10.count_ref, s32[64]{0:T(128)} %get-tuple-element.38.row_ref, s32[64]{0:T(128)} %get-tuple-element.44.group_ref, s32[64]{0:T(128)} %get-tuple-element.34.sub_ref, f32[64]{0:T(128)} %copy-done.4, ...), custom_call_target="tpu_custom_call" | custom-call | flops 4831838208 | bytes 6324224 | tf_op jit(solution)/shard_map/pallas_call | solution.py:123
  139.9 4.4 %collective-permute-done.2 = f32[2,1032,256]{2,1,0:T(8,128)S(1)} collective-permute-done((f32[2,1032,256]{2,1,0:T(8,128)}, f32[2,1032,256]{2,1,0:T(8,128)S(1)}, u32[]{:S(2)}, u32[]{:S(2)}) %collective-permute-start.2) | collective-permute-done | bytes 2113568 | tf_op jit(solution)/shard_map/ppermute | solution.py:148
  144.3 1.9 %add.111 = f32[2,1032,256]{2,1,0:T(8,128)S(1)} add(f32[2,1032,256]{2,1,0:T(8,128)} %get-tuple-element.18, f32[2,1032,256]{2,1,0:T(8,128)S(1)} %collective-permute-done.2) | non-fusion elementwise | flops 528384 | bytes 6340608 | tf_op jit(solution)/shard_map/add | solution.py:148
  146.9 24.8 %collective-permute-done.3 = f32[1,1032,256]{2,1,0:T(8,128)S(1)} collective-permute-done((f32[1,1032,256]{2,1,0:T(8,128)S(1)}, f32[1,1032,256]{2,1,0:T(8,128)S(1)}, u32[]{:S(2)}, u32[]{:S(2)}) %collective-permute-start.3) | collective-permute-done | bytes 1056800 | tf_op jit(solution)/shard_map/ppermute | solution.py:148
  172.5 0.6 fusion.32
  174.5 1.7 fusion.8
  (64 shorter events, 8.4 us)
Async XLA Ops:
  0.6 82.6 %copy-start = (bf16[9,41]{1,0:T(8,128)(2,1)S(1)}, bf16[9,41]{1,0:T(8,128)(2,1)}, u32[]{:S(2)}) copy-start(bf16[9,41]{1,0:T(8,128)(2,1)} %param.12) | copy-start | bytes 2218
  8.0 59.6 %all-to-all-start = ((bf16[8,8,144,128]{3,2,1,0:T(8,128)(2,1)}), bf16[8,8,144,128]{3,2,1,0:T(8,128)(2,1)S(1)}, u32[]{:S(2)}, u32[]{:S(2)}) async-start(bf16[8,8,144,128]{3,2,1,0:T(8,128)(2,1)} %bitcast.60), calls=%async_computation | async-start | bytes 4718592 | tf_op jit(solution)/shard_map/all_to_all | solution.py:198
  67.7 2.5 %copy-start.1 = (bf16[8,8,144,128]{3,2,1,0:T(8,128)(2,1)}, bf16[8,8,144,128]{3,2,1,0:T(8,128)(2,1)S(1)}, u32[]{:S(2)}) copy-start(bf16[8,8,144,128]{3,2,1,0:T(8,128)(2,1)S(1)} %all-to-all-done) | copy-start | bytes 7077892
  69.6 17.5 %copy-start.4 = (f32[64]{0:T(128)}, f32[64]{0:T(128)S(1)}, u32[]{:S(2)}) copy-start(f32[64]{0:T(128)S(1)} %get-tuple-element.33.w_ref) | copy-start | bytes 772
  70.2 52.2 %all-to-all-start.1 = ((bf16[8,8,128,128]{3,2,1,0:T(8,128)(2,1)}), bf16[8,8,128,128]{3,2,1,0:T(8,128)(2,1)}, u32[]{:S(2)}, u32[]{:S(2)}) async-start(bf16[8,8,128,128]{3,2,1,0:T(8,128)(2,1)} %bitcast.61), calls=%async_computation.1 | async-start | bytes 4194304 | tf_op jit(solution)/shard_map/all_to_all | solution.py:238
  76.2 9.0 %copy-start.5 = (bf16[9,41]{1,0:T(8,128)(2,1)S(1)}, bf16[9,41]{1,0:T(8,128)(2,1)}, u32[]{:S(2)}) copy-start(bf16[9,41]{1,0:T(8,128)(2,1)} %param.13) | copy-start | bytes 2218
  83.2 4.8 %collective-permute-start = (f32[2,1024,256]{2,1,0:T(8,128)}, f32[2,1024,256]{2,1,0:T(8,128)S(1)}, u32[]{:S(2)}, u32[]{:S(2)}) collective-permute-start(f32[2,1024,256]{2,1,0:T(8,128)} %get-tuple-element.15), channel_id=1, source_target_pairs={{0,1},{1,0},{2,3},{3,2},{4,5},{5,4},{6,7},{7,6},{8,9},{9,8},{10,11... | collective-permute-start | bytes 6291464 | tf_op jit(solution)/shard_map/ppermute | solution.py:148
  88.0 1.4 copy-start.2
  91.9 1.8 %copy-start.3 = (s32[64]{0:T(128)S(1)}, s32[64]{0:T(128)}, u32[]{:S(2)}) copy-start(s32[64]{0:T(128)} %get-tuple-element.38.row_ref) | copy-start | bytes 772
  92.0 25.7 %collective-permute-start.1 = (f32[1,1024,256]{2,1,0:T(8,128)S(1)}, f32[1,1024,256]{2,1,0:T(8,128)}, u32[]{:S(2)}, u32[]{:S(2)}) collective-permute-start(f32[1,1024,256]{2,1,0:T(8,128)S(1)} %slice.68), channel_id=1, source_target_pairs={{0,2},{1,3},{2,0},{3,1},{4,6},{5,7},{6,4},{7,5},{8,10},{9,11},{10,... | collective-permute-start | bytes 3145736 | tf_op jit(solution)/shard_map/ppermute | solution.py:148
  139.9 4.4 %collective-permute-start.2 = (f32[2,1032,256]{2,1,0:T(8,128)}, f32[2,1032,256]{2,1,0:T(8,128)S(1)}, u32[]{:S(2)}, u32[]{:S(2)}) collective-permute-start(f32[2,1032,256]{2,1,0:T(8,128)} %get-tuple-element.19), channel_id=1, source_target_pairs={{0,1},{1,0},{2,3},{3,2},{4,5},{5,4},{6,7},{7,6},{8,9},{9,8},{10,11... | collective-permute-start | bytes 6340616 | tf_op jit(solution)/shard_map/ppermute | solution.py:148
  146.3 25.4 %collective-permute-start.3 = (f32[1,1032,256]{2,1,0:T(8,128)S(1)}, f32[1,1032,256]{2,1,0:T(8,128)S(1)}, u32[]{:S(2)}, u32[]{:S(2)}) collective-permute-start(f32[1,1032,256]{2,1,0:T(8,128)S(1)} %slice.70), channel_id=1, source_target_pairs={{0,2},{1,3},{2,0},{3,1},{4,6},{5,7},{6,4},{7,5},{8,10},{9,11},{10,... | collective-permute-start | bytes 3170312 | tf_op jit(solution)/shard_map/ppermute | solution.py:148

commit v4 on v3

--- a/solution.py
+++ b/solution.py
@@ -9,7 +9,7 @@
 BASIS = 9
 META = 16
 EXTRA = 8
-GANG = 4
+GANG = 8
 
 
 weight_floor = 0.5

time: 175 us -> 174 us (level)
  the two profiles are of different devices: /device:TPU:6 before, /device:TPU:24 now
where the time goes in v4:
time: 174 us; the launch traced here: 170 us
  waiting for transfers between devices  99.6 us (57%)
  other arithmetic  20 us (11%)
  Pallas kernels  19.7 us (11%)
  starting transfers between devices  14.7 us (8%)
  local copies, waits for them, and re-layouts  14 us (8%)
    all_to_all x1, waiting for transfers between devices, shards(): lax.all_to_all(send_vm, 'sky', split_axis=0, concat_axis=0, tiled=True)  48.9 us
    ppermute x4, waiting for transfers between devices, reduce_scatter_visit(): field = keep + lax.ppermute(send, 'visit', perm=pairs)  48.2 us
    pallas_call x1, Pallas kernels, image_field(): pl.pallas_call(image_kernel, out_shape=halves_of(field_shape), in_specs=[...  13.2 us
    pallas_call x1, Pallas kernels, variance_field(): pl.pallas_call(variance_kernel, out_shape=halves_of(field_shape), in_spec...  6.44 us
    all_to_all x1, starting transfers between devices, shards(): lax.all_to_all(send_vm, 'sky', split_axis=0, concat_axis=0, tiled=True)  6.03 us
    all_to_all x1, starting transfers between devices, shards(): lax.all_to_all(send_im, 'sky', split_axis=0, concat_axis=0, tiled=True)  5.8 us
    add x3, other arithmetic, reduce_scatter_visit(): field = keep + lax.ppermute(send, 'visit', perm=pairs)  4.56 us
    gather x2, local copies, waits for them, and re-layouts, gather_slots(): jnp.take(padded, source_tile, axis=0, mode='clip')  4.4 us
  transfers between devices with their start and end apart: 6, of which 5 were waited for; matrix products, arithmetic and copies ran while one was open for 11% of the time, Pallas kernels for 4%

profile of v4, /device:TPU:24, one launch (start us, length us, event | category | flops | bytes accessed | tf_op | source)
XLA Modules:
  0.0 170.4 jit_solution(1213511928545618706)
XLA Ops:
  0.6 0.9 convert_reduce_fusion.2
  1.6 0.7 multiply_add_fusion.1
  3.1 0.8 copy.28
  4.2 1.5 maximum_maximum_fusion
  5.8 2.3 %gather_fusion = bf16[64,144,128]{2,1,0:T(8,128)(2,1)} fusion(bf16[33,144,128]{2,1,0:T(8,128)(2,1)S(1)} %concatenate.23, s32[1024]{0:T(1024)S(1)} %pad_clamp_fusion.1), kind=kCustom, calls=%fused_computation | custom fusion | bytes 4718848 | tf_op jit(solution)/shard_map/jit(_take)/gather | solution.py:191
  8.0 6.0 %all-to-all-start = ((bf16[8,8,144,128]{3,2,1,0:T(8,128)(2,1)}), bf16[8,8,144,128]{3,2,1,0:T(8,128)(2,1)S(1)}, u32[]{:S(2)}, u32[]{:S(2)}) async-start(bf16[8,8,144,128]{3,2,1,0:T(8,128)(2,1)} %bitcast.60), calls=%async_computation | async-start | bytes 4718592 | tf_op jit(solution)/shard_map/all_to_all | solution.py:198
  14.1 1.3 concatenate.24
  15.4 2.1 %gather_fusion.1 = bf16[64,128,128]{2,1,0:T(8,128)(2,1)} fusion(bf16[33,128,128]{2,1,0:T(8,128)(2,1)S(1)} %concatenate.24, s32[1024]{0:T(1024)S(1)} %pad_clamp_fusion.1), kind=kCustom, calls=%fused_computation.1 | custom fusion | bytes 4194560 | tf_op jit(solution)/shard_map/jit(_take)/gather | solution.py:191
  17.5 48.9 %all-to-all-done = bf16[8,8,144,128]{3,2,1,0:T(8,128)(2,1)S(1)} async-done(((bf16[8,8,144,128]{3,2,1,0:T(8,128)(2,1)}), bf16[8,8,144,128]{3,2,1,0:T(8,128)(2,1)S(1)}, u32[]{:S(2)}, u32[]{:S(2)}) %all-to-all-start) | async-done | bytes 2359328 | tf_op jit(solution)/shard_map/all_to_all | solution.py:198
  68.9 5.8 %all-to-all-start.1 = ((bf16[8,8,128,128]{3,2,1,0:T(8,128)(2,1)}), bf16[8,8,128,128]{3,2,1,0:T(8,128)(2,1)}, u32[]{:S(2)}, u32[]{:S(2)}) async-start(bf16[8,8,128,128]{3,2,1,0:T(8,128)(2,1)} %bitcast.61), calls=%async_computation.1 | async-start | bytes 4194304 | tf_op jit(solution)/shard_map/all_to_all | solution.py:238
  74.7 1.3 fusion.31
  75.9 6.4 %shard_map.94 = (f32[2,1024,256]{2,1,0:T(8,128)}, f32[2,1024,256]{2,1,0:T(8,128)}) custom-call(s32[64]{0:T(128)} %get-tuple-element.38.row_ref, s32[64]{0:T(128)} %get-tuple-element.44.group_ref, s32[64]{0:T(128)} %get-tuple-element.34.sub_ref, f32[64]{0:T(128)} %mul.54.w2_ref, bf16[64,144,128]{2,1,0:T(8,128)(2,1)} %bitcast.59), custom_call_target="tpu_custom_call" | custom-call | tf_op jit(solution)/shard_map/pallas_call | solution.py:111
  82.4 0.7 fusion.7
  83.5 0.9 copy.35.row_side_ref
  84.4 0.7 fusion.6
  85.2 0.9 copy.36.col_side_ref
  87.2 1.3 copy-done.2
  88.6 2.5 %add.106 = f32[2,1024,256]{2,1,0:T(8,128)S(1)} add(f32[2,1024,256]{2,1,0:T(8,128)} %get-tuple-element.14, f32[2,1024,256]{2,1,0:T(8,128)} %copy-done.2) | non-fusion elementwise | flops 524288 | bytes 6291456 | tf_op jit(solution)/shard_map/add | solution.py:148
  91.1 1.4 collective-permute-start.1
  92.9 0.7 reshape.184.coef_ref
  93.7 2.1 %sort.17 = (pred[64]{0:T(512)(128)(4,1)}, s32[64]{0:T(128)}) sort(pred[64]{0:T(512)(128)(4,1)S(1)} %compare_not_fusion, s32[64]{0:T(128)S(1)} %iota.46), dimensions={0}, to_apply=%region_3.4 | sort | flops 384 | bytes 640 | tf_op jit(solution)/shard_map/jit(argsort)/sort | solution.py:121
  95.7 0.7 pad_maximum_fusion
  96.4 0.7 maximum_maximum_fusion.1.extra_ref
  97.1 19.8 %collective-permute-done.1 = f32[1,1024,256]{2,1,0:T(8,128)} collective-permute-done((f32[1,1024,256]{2,1,0:T(8,128)S(1)}, f32[1,1024,256]{2,1,0:T(8,128)}, u32[]{:S(2)}, u32[]{:S(2)}) %collective-permute-start.1) | collective-permute-done | bytes 1048608 | tf_op jit(solution)/shard_map/ppermute | solution.py:148
  116.9 1.4 fusion.9
  118.3 2.6 %all-to-all-done.1 = bf16[8,8,128,128]{3,2,1,0:T(8,128)(2,1)} async-done(((bf16[8,8,128,128]{3,2,1,0:T(8,128)(2,1)}), bf16[8,8,128,128]{3,2,1,0:T(8,128)(2,1)}, u32[]{:S(2)}, u32[]{:S(2)}) %all-to-all-start.1) | async-done | bytes 2097184 | tf_op jit(solution)/shard_map/all_to_all | solution.py:238
  120.9 13.2 %shard_map.95 = (f32[2,1032,256]{2,1,0:T(8,128)}, f32[2,1032,256]{2,1,0:T(8,128)}) custom-call(s32[64]{0:T(128)} %get-tuple-element.13.order_ref, s32[1]{0:T(128)} %bitcast.10.count_ref, s32[64]{0:T(128)} %get-tuple-element.38.row_ref, s32[64]{0:T(128)} %get-tuple-element.44.group_ref, s32[64]{0:T(128)} %get-tuple-element.34.sub_ref, f32[64]{0:T(128)} %copy-done.4, ...), custom_call_target="tpu_custom_call" | custom-call | flops 4831838208 | bytes 6324224 | tf_op jit(solution)/shard_map/pallas_call | solution.py:123
  134.1 4.4 %collective-permute-done.2 = f32[2,1032,256]{2,1,0:T(8,128)S(1)} collective-permute-done((f32[2,1032,256]{2,1,0:T(8,128)}, f32[2,1032,256]{2,1,0:T(8,128)S(1)}, u32[]{:S(2)}, u32[]{:S(2)}) %collective-permute-start.2) | collective-permute-done | bytes 2113568 | tf_op jit(solution)/shard_map/ppermute | solution.py:148
  138.5 1.9 %add.111 = f32[2,1032,256]{2,1,0:T(8,128)S(1)} add(f32[2,1032,256]{2,1,0:T(8,128)} %get-tuple-element.18, f32[2,1032,256]{2,1,0:T(8,128)S(1)} %collective-permute-done.2) | non-fusion elementwise | flops 528384 | bytes 6340608 | tf_op jit(solution)/shard_map/add | solution.py:148
  140.5 1.4 collective-permute-start.3
  142.0 24.0 %collective-permute-done.3 = f32[1,1032,256]{2,1,0:T(8,128)S(1)} collective-permute-done((f32[1,1032,256]{2,1,0:T(8,128)S(1)}, f32[1,1032,256]{2,1,0:T(8,128)S(1)}, u32[]{:S(2)}, u32[]{:S(2)}) %collective-permute-start.3) | collective-permute-done | bytes 1056800 | tf_op jit(solution)/shard_map/ppermute | solution.py:148
  168.7 1.7 %fusion.8 = (f32[1024,256]{1,0:T(8,128)}, f32[1024,256]{1,0:T(8,128)}) fusion(f32[1024,256]{1,0:T(8,128)S(1)} %fusion.9, f32[128,8,2,128]{3,2,1,0:T(2,128)S(1)} %bitcast.64, f32[1,1032,256]{2,1,0:T(8,128)S(1)} %slice_add_fusion), kind=kLoop, calls=%fused_computation.18 | loop fusion | flops 786432 | bytes 5242880 | tf_op jit(solution)/shard_map/div | solution.py:253
  (64 shorter events, 8.5 us)
Async XLA Ops:
  0.6 81.8 %copy-start = (bf16[9,41]{1,0:T(8,128)(2,1)S(1)}, bf16[9,41]{1,0:T(8,128)(2,1)}, u32[]{:S(2)}) copy-start(bf16[9,41]{1,0:T(8,128)(2,1)} %param.12) | copy-start | bytes 2218
  8.0 58.3 %all-to-all-start = ((bf16[8,8,144,128]{3,2,1,0:T(8,128)(2,1)}), bf16[8,8,144,128]{3,2,1,0:T(8,128)(2,1)S(1)}, u32[]{:S(2)}, u32[]{:S(2)}) async-start(bf16[8,8,144,128]{3,2,1,0:T(8,128)(2,1)} %bitcast.60), calls=%async_computation | async-start | bytes 4718592 | tf_op jit(solution)/shard_map/all_to_all | solution.py:198
  66.4 2.5 %copy-start.1 = (bf16[8,8,144,128]{3,2,1,0:T(8,128)(2,1)}, bf16[8,8,144,128]{3,2,1,0:T(8,128)(2,1)S(1)}, u32[]{:S(2)}) copy-start(bf16[8,8,144,128]{3,2,1,0:T(8,128)(2,1)S(1)} %all-to-all-done) | copy-start | bytes 7077892
  68.3 17.9 %copy-start.4 = (f32[64]{0:T(128)}, f32[64]{0:T(128)S(1)}, u32[]{:S(2)}) copy-start(f32[64]{0:T(128)S(1)} %get-tuple-element.33.w_ref) | copy-start | bytes 772
  68.9 52.1 %all-to-all-start.1 = ((bf16[8,8,128,128]{3,2,1,0:T(8,128)(2,1)}), bf16[8,8,128,128]{3,2,1,0:T(8,128)(2,1)}, u32[]{:S(2)}, u32[]{:S(2)}) async-start(bf16[8,8,128,128]{3,2,1,0:T(8,128)(2,1)} %bitcast.61), calls=%async_computation.1 | async-start | bytes 4194304 | tf_op jit(solution)/shard_map/all_to_all | solution.py:238
  75.9 8.4 %copy-start.5 = (bf16[9,41]{1,0:T(8,128)(2,1)S(1)}, bf16[9,41]{1,0:T(8,128)(2,1)}, u32[]{:S(2)}) copy-start(bf16[9,41]{1,0:T(8,128)(2,1)} %param.13) | copy-start | bytes 2218
  82.4 4.8 %collective-permute-start = (f32[2,1024,256]{2,1,0:T(8,128)}, f32[2,1024,256]{2,1,0:T(8,128)S(1)}, u32[]{:S(2)}, u32[]{:S(2)}) collective-permute-start(f32[2,1024,256]{2,1,0:T(8,128)} %get-tuple-element.15), channel_id=1, source_target_pairs={{0,1},{1,0},{2,3},{3,2},{4,5},{5,4},{6,7},{7,6},{8,9},{9,8},{10,11... | collective-permute-start | bytes 6291464 | tf_op jit(solution)/shard_map/ppermute | solution.py:148
  87.2 1.4 copy-start.2
  91.0 2.6 %copy-start.3 = (s32[64]{0:T(128)S(1)}, s32[64]{0:T(128)}, u32[]{:S(2)}) copy-start(s32[64]{0:T(128)} %get-tuple-element.38.row_ref) | copy-start | bytes 772
  91.1 25.7 %collective-permute-start.1 = (f32[1,1024,256]{2,1,0:T(8,128)S(1)}, f32[1,1024,256]{2,1,0:T(8,128)}, u32[]{:S(2)}, u32[]{:S(2)}) collective-permute-start(f32[1,1024,256]{2,1,0:T(8,128)S(1)} %slice.68), channel_id=1, source_target_pairs={{0,2},{1,3},{2,0},{3,1},{4,6},{5,7},{6,4},{7,5},{8,10},{9,11},{10,... | collective-permute-start | bytes 3145736 | tf_op jit(solution)/shard_map/ppermute | solution.py:148
  134.1 4.4 %collective-permute-start.2 = (f32[2,1032,256]{2,1,0:T(8,128)}, f32[2,1032,256]{2,1,0:T(8,128)S(1)}, u32[]{:S(2)}, u32[]{:S(2)}) collective-permute-start(f32[2,1032,256]{2,1,0:T(8,128)} %get-tuple-element.19), channel_id=1, source_target_pairs={{0,1},{1,0},{2,3},{3,2},{4,5},{5,4},{6,7},{7,6},{8,9},{9,8},{10,11... | collective-permute-start | bytes 6340616 | tf_op jit(solution)/shard_map/ppermute | solution.py:148
  140.5 25.4 %collective-permute-start.3 = (f32[1,1032,256]{2,1,0:T(8,128)S(1)}, f32[1,1032,256]{2,1,0:T(8,128)S(1)}, u32[]{:S(2)}, u32[]{:S(2)}) collective-permute-start(f32[1,1032,256]{2,1,0:T(8,128)S(1)} %slice.70), channel_id=1, source_target_pairs={{0,2},{1,3},{2,0},{3,1},{4,6},{5,7},{6,4},{7,5},{8,10},{9,11},{10,... | collective-permute-start | bytes 3170312 | tf_op jit(solution)/shard_map/ppermute | solution.py:148

commit v5 on v3

--- a/solution.py
+++ b/solution.py
@@ -145,10 +145,12 @@
     keep, send = halves
     for b in range(bits):
         pairs = [(i, i ^ (1 << b)) for i in range(n_visit)]
-        field = keep + lax.ppermute(send, "visit", perm=pairs)
-        half = field.shape[0] // 2
-        keep, send = field[:half], field[half:]
-    return field[0]
+        got = lax.ppermute(send, "visit", perm=pairs)
+        half = keep.shape[0] // 2
+        if half == 0:
+            return (keep + got)[0]
+        send = keep[half:] + got[half:]
+        keep = keep[:half] + got[:half]
 
 
 def shards(tile_image, tile_variance, match_coeffs, tile_patch, tile_offset, row_taps, col_taps):

time: 175 us -> 183 us (1.046)
  the two profiles are of different devices: /device:TPU:6 before, /device:TPU:24 now
where the time goes in v5:
time: 183 us; the launch traced here: 180 us
  waiting for transfers between devices  110 us (60%)
  Pallas kernels  20.4 us (11%)
  other arithmetic  19.2 us (10%)
  starting transfers between devices  14 us (8%)
  local copies, waits for them, and re-layouts  13.8 us (8%)
    all_to_all x1, waiting for transfers between devices, shards(): lax.all_to_all(send_vm, 'sky', split_axis=0, concat_axis=0, tiled=True)  48.9 us
    ppermute x4, waiting for transfers between devices, reduce_scatter_visit(): got = lax.ppermute(send, 'visit', perm=pairs)  47.6 us
    pallas_call x1, Pallas kernels, image_field(): pl.pallas_call(image_kernel, out_shape=halves_of(field_shape), in_specs=[...  14.1 us
    all_to_all x1, waiting for transfers between devices, shards(): lax.all_to_all(send_im, 'sky', split_axis=0, concat_axis=0, tiled=True)  13.6 us
    pallas_call x1, Pallas kernels, variance_field(): pl.pallas_call(variance_kernel, out_shape=halves_of(field_shape), in_spec...  6.3 us
    all_to_all x1, starting transfers between devices, shards(): lax.all_to_all(send_vm, 'sky', split_axis=0, concat_axis=0, tiled=True)  6.03 us
    all_to_all x1, starting transfers between devices, shards(): lax.all_to_all(send_im, 'sky', split_axis=0, concat_axis=0, tiled=True)  5.1 us
    gather x2, local copies, waits for them, and re-layouts, gather_slots(): jnp.take(padded, source_tile, axis=0, mode='clip')  4.4 us
  transfers between devices with their start and end apart: 6, of which 5 were waited for; matrix products, arithmetic and copies ran while one was open for 9% of the time, Pallas kernels for 0%

profile of v5, /device:TPU:24, one launch (start us, length us, event | category | flops | bytes accessed | tf_op | source)
XLA Modules:
  0.0 179.9 jit_solution(18429905972187625699)
XLA Ops:
  0.6 0.9 convert_reduce_fusion.2
  3.1 0.8 copy.28
  4.2 1.5 maximum_maximum_fusion
  5.8 2.3 %gather_fusion = bf16[64,144,128]{2,1,0:T(8,128)(2,1)} fusion(bf16[33,144,128]{2,1,0:T(8,128)(2,1)S(1)} %concatenate.23, s32[1024]{0:T(1024)S(1)} %pad_clamp_fusion.1), kind=kCustom, calls=%fused_computation | custom fusion | bytes 4718848 | tf_op jit(solution)/shard_map/jit(_take)/gather | solution.py:193
  8.0 6.0 %all-to-all-start = ((bf16[8,8,144,128]{3,2,1,0:T(8,128)(2,1)}), bf16[8,8,144,128]{3,2,1,0:T(8,128)(2,1)S(1)}, u32[]{:S(2)}, u32[]{:S(2)}) async-start(bf16[8,8,144,128]{3,2,1,0:T(8,128)(2,1)} %bitcast.60), calls=%async_computation | async-start | bytes 4718592 | tf_op jit(solution)/shard_map/all_to_all | solution.py:200
  14.1 1.3 concatenate.24
  15.4 2.1 %gather_fusion.1 = bf16[64,128,128]{2,1,0:T(8,128)(2,1)} fusion(bf16[33,128,128]{2,1,0:T(8,128)(2,1)S(1)} %concatenate.24, s32[1024]{0:T(1024)S(1)} %pad_clamp_fusion.1), kind=kCustom, calls=%fused_computation.1 | custom fusion | bytes 4194560 | tf_op jit(solution)/shard_map/jit(_take)/gather | solution.py:193
  17.5 48.9 %all-to-all-done = bf16[8,8,144,128]{3,2,1,0:T(8,128)(2,1)S(1)} async-done(((bf16[8,8,144,128]{3,2,1,0:T(8,128)(2,1)}), bf16[8,8,144,128]{3,2,1,0:T(8,128)(2,1)S(1)}, u32[]{:S(2)}, u32[]{:S(2)}) %all-to-all-start) | async-done | bytes 2359328 | tf_op jit(solution)/shard_map/all_to_all | solution.py:200
  67.7 0.7 fusion.35
  68.9 1.1 fusion.33
  70.0 6.3 %shard_map.94 = (f32[2,1024,256]{2,1,0:T(8,128)}, f32[2,1024,256]{2,1,0:T(8,128)}) custom-call(s32[64]{0:T(128)} %get-tuple-element.38.row_ref, s32[64]{0:T(128)} %get-tuple-element.44.group_ref, s32[64]{0:T(128)} %get-tuple-element.34.sub_ref, f32[64]{0:T(128)} %mul.54.w2_ref, bf16[64,144,128]{2,1,0:T(8,128)(2,1)} %bitcast.59), custom_call_target="tpu_custom_call" | custom-call | tf_op jit(solution)/shard_map/pallas_call | solution.py:111
  76.3 5.1 %all-to-all-start.1 = ((bf16[8,8,128,128]{3,2,1,0:T(8,128)(2,1)}), bf16[8,8,128,128]{3,2,1,0:T(8,128)(2,1)S(1)}, u32[]{:S(2)}, u32[]{:S(2)}) async-start(bf16[8,8,128,128]{3,2,1,0:T(8,128)(2,1)} %bitcast.61), calls=%async_computation.1 | async-start | bytes 4194304 | tf_op jit(solution)/shard_map/all_to_all | solution.py:240
  81.5 0.7 fusion.7
  82.5 0.9 copy.35.row_side_ref
  83.4 0.7 fusion.6
  84.2 0.9 copy.36.col_side_ref
  86.3 1.7 slice_add_fusion.2
  87.9 1.6 collective-permute-start.1
  89.9 0.7 reshape.184.coef_ref
  90.7 2.1 %sort.17 = (pred[64]{0:T(512)(128)(4,1)}, s32[64]{0:T(128)}) sort(pred[64]{0:T(512)(128)(4,1)S(1)} %compare_not_fusion, s32[64]{0:T(128)S(1)} %iota.46), dimensions={0}, to_apply=%region_3.4 | sort | flops 384 | bytes 640 | tf_op jit(solution)/shard_map/jit(argsort)/sort | solution.py:121
  92.8 0.7 pad_maximum_fusion
  93.5 0.7 maximum_maximum_fusion.1.extra_ref
  94.1 19.0 %collective-permute-done.1 = f32[1,1024,256]{2,1,0:T(8,128)} collective-permute-done((f32[1,1024,256]{2,1,0:T(8,128)S(1)}, f32[1,1024,256]{2,1,0:T(8,128)}, u32[]{:S(2)}, u32[]{:S(2)}) %collective-permute-start.1) | collective-permute-done | bytes 1048608 | tf_op jit(solution)/shard_map/ppermute | solution.py:148
  113.1 2.1 %fusion.11 = f32[1024,256]{1,0:T(8,128)S(1)} fusion(f32[1,1024,256]{2,1,0:T(8,128)} %collective-permute-done.1, f32[2,1024,256]{2,1,0:T(8,128)} %collective-permute-done, f32[2,1024,256]{2,1,0:T(8,128)} %get-tuple-element.14), kind=kLoop, calls=%fused_computation.25 | loop fusion | flops 524288 | bytes 4194304 | tf_op jit(solution)/shard_map/squeeze | solution.py:151
  115.2 13.6 %all-to-all-done.1 = bf16[8,8,128,128]{3,2,1,0:T(8,128)(2,1)S(1)} async-done(((bf16[8,8,128,128]{3,2,1,0:T(8,128)(2,1)}), bf16[8,8,128,128]{3,2,1,0:T(8,128)(2,1)S(1)}, u32[]{:S(2)}, u32[]{:S(2)}) %all-to-all-start.1) | async-done | bytes 2097184 | tf_op jit(solution)/shard_map/all_to_all | solution.py:240
  128.8 1.3 copy-done.3
  130.1 14.1 %shard_map.95 = (f32[2,1032,256]{2,1,0:T(8,128)}, f32[2,1032,256]{2,1,0:T(8,128)}) custom-call(s32[64]{0:T(128)} %get-tuple-element.13.order_ref, s32[1]{0:T(128)} %bitcast.10.count_ref, s32[64]{0:T(128)} %get-tuple-element.38.row_ref, s32[64]{0:T(128)} %get-tuple-element.44.group_ref, s32[64]{0:T(128)} %get-tuple-element.34.sub_ref, f32[64]{0:T(128)} %copy-done.5, ...), custom_call_target="tpu_custom_call" | custom-call | flops 4831838208 | bytes 6324224 | tf_op jit(solution)/shard_map/pallas_call | solution.py:123
  144.2 4.4 %collective-permute-done.2 = f32[2,1032,256]{2,1,0:T(8,128)S(1)} collective-permute-done((f32[2,1032,256]{2,1,0:T(8,128)}, f32[2,1032,256]{2,1,0:T(8,128)S(1)}, u32[]{:S(2)}, u32[]{:S(2)}) %collective-permute-start.2) | collective-permute-done | bytes 2113568 | tf_op jit(solution)/shard_map/ppermute | solution.py:148
  148.6 1.3 slice_add_fusion
  150.0 1.2 collective-permute-start.3
  151.2 24.2 %collective-permute-done.3 = f32[1,1032,256]{2,1,0:T(8,128)S(1)} collective-permute-done((f32[1,1032,256]{2,1,0:T(8,128)S(1)}, f32[1,1032,256]{2,1,0:T(8,128)S(1)}, u32[]{:S(2)}, u32[]{:S(2)}) %collective-permute-start.3) | collective-permute-done | bytes 1056800 | tf_op jit(solution)/shard_map/ppermute | solution.py:148
  178.2 1.7 fusion.9
  (64 shorter events, 8.5 us)
Async XLA Ops:
  0.6 80.8 %copy-start = (bf16[9,41]{1,0:T(8,128)(2,1)S(1)}, bf16[9,41]{1,0:T(8,128)(2,1)}, u32[]{:S(2)}) copy-start(bf16[9,41]{1,0:T(8,128)(2,1)} %param.12) | copy-start | bytes 2218
  8.0 58.3 %all-to-all-start = ((bf16[8,8,144,128]{3,2,1,0:T(8,128)(2,1)}), bf16[8,8,144,128]{3,2,1,0:T(8,128)(2,1)S(1)}, u32[]{:S(2)}, u32[]{:S(2)}) async-start(bf16[8,8,144,128]{3,2,1,0:T(8,128)(2,1)} %bitcast.60), calls=%async_computation | async-start | bytes 4718592 | tf_op jit(solution)/shard_map/all_to_all | solution.py:200
  66.4 3.7 %copy-start.1 = (bf16[8,8,144,128]{3,2,1,0:T(8,128)(2,1)}, bf16[8,8,144,128]{3,2,1,0:T(8,128)(2,1)S(1)}, u32[]{:S(2)}) copy-start(bf16[8,8,144,128]{3,2,1,0:T(8,128)(2,1)S(1)} %all-to-all-done) | copy-start | bytes 7077892
  68.4 17.0 %copy-start.5 = (f32[64]{0:T(128)}, f32[64]{0:T(128)S(1)}, u32[]{:S(2)}) copy-start(f32[64]{0:T(128)S(1)} %get-tuple-element.33.w_ref) | copy-start | bytes 772
  76.3 9.9 %collective-permute-start = (f32[2,1024,256]{2,1,0:T(8,128)}, f32[2,1024,256]{2,1,0:T(8,128)}, u32[]{:S(2)}, u32[]{:S(2)}) collective-permute-start(f32[2,1024,256]{2,1,0:T(8,128)} %get-tuple-element.15), channel_id=1, source_target_pairs={{0,1},{1,0},{2,3},{3,2},{4,5},{5,4},{6,7},{7,6},{8,9},{9,8},{10,11... | collective-permute-start | bytes 6291464 | tf_op jit(solution)/shard_map/ppermute | solution.py:148
  76.3 52.5 %all-to-all-start.1 = ((bf16[8,8,128,128]{3,2,1,0:T(8,128)(2,1)}), bf16[8,8,128,128]{3,2,1,0:T(8,128)(2,1)S(1)}, u32[]{:S(2)}, u32[]{:S(2)}) async-start(bf16[8,8,128,128]{3,2,1,0:T(8,128)(2,1)} %bitcast.61), calls=%async_computation.1 | async-start | bytes 4194304 | tf_op jit(solution)/shard_map/all_to_all | solution.py:240
  81.4 2.0 %copy-start.6 = (bf16[9,41]{1,0:T(8,128)(2,1)S(1)}, bf16[9,41]{1,0:T(8,128)(2,1)}, u32[]{:S(2)}) copy-start(bf16[9,41]{1,0:T(8,128)(2,1)} %param.13) | copy-start | bytes 2218
  84.2 6.4 %copy-start.4 = (s32[64]{0:T(128)S(1)}, s32[64]{0:T(128)}, u32[]{:S(2)}) copy-start(s32[64]{0:T(128)} %get-tuple-element.38.row_ref) | copy-start | bytes 772
  87.9 25.2 %collective-permute-start.1 = (f32[1,1024,256]{2,1,0:T(8,128)S(1)}, f32[1,1024,256]{2,1,0:T(8,128)}, u32[]{:S(2)}, u32[]{:S(2)}) collective-permute-start(f32[1,1024,256]{2,1,0:T(8,128)S(1)} %slice_add_fusion.2), channel_id=1, source_target_pairs={{0,2},{1,3},{2,0},{3,1},{4,6},{5,7},{6,4},{7,5},{8,10},{9,11},{10,... | collective-permute-start | bytes 3145736 | tf_op jit(solution)/shard_map/ppermute | solution.py:148
  128.8 1.3 copy-start.3
  144.2 31.2 %copy-start.2 = (f32[2,1032,256]{2,1,0:T(8,128)S(1)}, f32[2,1032,256]{2,1,0:T(8,128)}, u32[]{:S(2)}) copy-start(f32[2,1032,256]{2,1,0:T(8,128)} %get-tuple-element.18) | copy-start | bytes 6340612
  144.2 4.4 %collective-permute-start.2 = (f32[2,1032,256]{2,1,0:T(8,128)}, f32[2,1032,256]{2,1,0:T(8,128)S(1)}, u32[]{:S(2)}, u32[]{:S(2)}) collective-permute-start(f32[2,1032,256]{2,1,0:T(8,128)} %get-tuple-element.19), channel_id=1, source_target_pairs={{0,1},{1,0},{2,3},{3,2},{4,5},{5,4},{6,7},{7,6},{8,9},{9,8},{10,11... | collective-permute-start | bytes 6340616 | tf_op jit(solution)/shard_map/ppermute | solution.py:148
  150.0 25.4 %collective-permute-start.3 = (f32[1,1032,256]{2,1,0:T(8,128)S(1)}, f32[1,1032,256]{2,1,0:T(8,128)S(1)}, u32[]{:S(2)}, u32[]{:S(2)}) collective-permute-start(f32[1,1032,256]{2,1,0:T(8,128)S(1)} %slice_add_fusion), channel_id=1, source_target_pairs={{0,2},{1,3},{2,0},{3,1},{4,6},{5,7},{6,4},{7,5},{8,10},{9,11},{10,... | collective-permute-start | bytes 3170312 | tf_op jit(solution)/shard_map/ppermute | solution.py:148

commit v6 on v3

--- a/solution.py
+++ b/solution.py
@@ -68,7 +68,7 @@
 
     def body(p, carry):
         pair = tuple(order_ref[GANG * p + h] for h in range(GANG))
-        both = jnp.concatenate([img_ref[t] for t in pair], axis=0)
+        both = img_ref[pl.ds(GANG * p, GANG)].reshape(GANG * tile, tile)
         first = jnp.dot(both, row_side_ref[...], preferred_element_type=jnp.float32)
         blocks = []
         for k in range(BASIS):
@@ -130,7 +130,7 @@
             transcendentals=0,
             bytes_accessed=images.size * 2 + 4 * (field_shape[0] * field_shape[1] * field_shape[2]),
         ),
-    )(order, count, *where, w, coef, images, row_side, col_side, extra)
+    )(order, count, *where, w, coef, jnp.take(images, order, axis=0), row_side, col_side, extra)
 
 
 def bit_reverse(values, bits):

time: 175 us -> 179 us (1.023)
  the two profiles are of different devices: /device:TPU:6 before, /device:TPU:0 now
where the time goes in v6:
time: 179 us; the launch traced here: 178 us
  waiting for transfers between devices  103 us (58%)
  other arithmetic  21.6 us (12%)
  Pallas kernels  20.6 us (12%)
  local copies, waits for them, and re-layouts  16.5 us (9%)
  starting transfers between devices  14 us (8%)
    all_to_all x1, waiting for transfers between devices, shards(): lax.all_to_all(send_vm, 'sky', split_axis=0, concat_axis=0, tiled=True)  50.4 us
    ppermute x4, waiting for transfers between devices, reduce_scatter_visit(): field = keep + lax.ppermute(send, 'visit', perm=pairs)  49.6 us
    pallas_call x1, Pallas kernels, image_field(): pl.pallas_call(image_kernel, out_shape=halves_of(field_shape), in_specs=[...  14.2 us
    all_to_all x1, starting transfers between devices, shards(): lax.all_to_all(send_vm, 'sky', split_axis=0, concat_axis=0, tiled=True)  7.25 us
    pallas_call x1, Pallas kernels, variance_field(): pl.pallas_call(variance_kernel, out_shape=halves_of(field_shape), in_spec...  6.38 us
    add x3, other arithmetic, reduce_scatter_visit(): field = keep + lax.ppermute(send, 'visit', perm=pairs)  4.56 us
    gather x2, local copies, waits for them, and re-layouts, gather_slots(): jnp.take(padded, source_tile, axis=0, mode='clip')  4.4 us
    all_to_all x1, starting transfers between devices, shards(): lax.all_to_all(send_im, 'sky', split_axis=0, concat_axis=0, tiled=True)  4.35 us
  transfers between devices with their start and end apart: 6, of which 5 were waited for; matrix products, arithmetic and copies ran while one was open for 10% of the time, Pallas kernels for 4%

profile of v6, /device:TPU:0, one launch (start us, length us, event | category | flops | bytes accessed | tf_op | source)
XLA Modules:
  0.0 178.4 jit_solution(9842128233244803713)
XLA Ops:
  0.6 0.9 convert_reduce_fusion.2
  3.1 0.8 copy.28
  4.2 1.5 maximum_maximum_fusion
  5.8 2.3 %gather_fusion = bf16[64,144,128]{2,1,0:T(8,128)(2,1)} fusion(bf16[33,144,128]{2,1,0:T(8,128)(2,1)S(1)} %concatenate.23, s32[1024]{0:T(1024)S(1)} %pad_clamp_fusion.2), kind=kCustom, calls=%fused_computation | custom fusion | bytes 4718848 | tf_op jit(solution)/shard_map/jit(_take)/gather | solution.py:191
  8.0 7.3 %all-to-all-start = ((bf16[8,8,144,128]{3,2,1,0:T(8,128)(2,1)}), bf16[8,8,144,128]{3,2,1,0:T(8,128)(2,1)S(1)}, u32[]{:S(2)}, u32[]{:S(2)}) async-start(bf16[8,8,144,128]{3,2,1,0:T(8,128)(2,1)} %bitcast.60), calls=%async_computation | async-start | bytes 4718592 | tf_op jit(solution)/shard_map/all_to_all | solution.py:198
  15.3 1.3 concatenate.24
  16.6 2.1 %gather_fusion.1 = bf16[64,128,128]{2,1,0:T(8,128)(2,1)} fusion(bf16[33,128,128]{2,1,0:T(8,128)(2,1)S(1)} %concatenate.24, s32[1024]{0:T(1024)S(1)} %pad_clamp_fusion.2), kind=kCustom, calls=%fused_computation.1 | custom fusion | bytes 4194560 | tf_op jit(solution)/shard_map/jit(_take)/gather | solution.py:191
  18.7 50.4 %all-to-all-done = bf16[8,8,144,128]{3,2,1,0:T(8,128)(2,1)S(1)} async-done(((bf16[8,8,144,128]{3,2,1,0:T(8,128)(2,1)}), bf16[8,8,144,128]{3,2,1,0:T(8,128)(2,1)S(1)}, u32[]{:S(2)}, u32[]{:S(2)}) %all-to-all-start) | async-done | bytes 2359328 | tf_op jit(solution)/shard_map/all_to_all | solution.py:198
  71.6 4.3 %all-to-all-start.1 = ((bf16[8,8,128,128]{3,2,1,0:T(8,128)(2,1)}), bf16[8,8,128,128]{3,2,1,0:T(8,128)(2,1)}, u32[]{:S(2)}, u32[]{:S(2)}) async-start(bf16[8,8,128,128]{3,2,1,0:T(8,128)(2,1)} %bitcast.61), calls=%async_computation.1 | async-start | bytes 4194304 | tf_op jit(solution)/shard_map/all_to_all | solution.py:238
  76.0 1.2 fusion.31
  77.2 6.4 %shard_map.94 = (f32[2,1024,256]{2,1,0:T(8,128)}, f32[2,1024,256]{2,1,0:T(8,128)}) custom-call(s32[64]{0:T(128)} %get-tuple-element.38.row_ref, s32[64]{0:T(128)} %get-tuple-element.44.group_ref, s32[64]{0:T(128)} %get-tuple-element.34.sub_ref, f32[64]{0:T(128)} %mul.54.w2_ref, bf16[64,144,128]{2,1,0:T(8,128)(2,1)} %bitcast.59), custom_call_target="tpu_custom_call" | custom-call | tf_op jit(solution)/shard_map/pallas_call | solution.py:111
  83.6 0.7 fusion.7
  84.7 0.9 copy.35.row_side_ref
  85.6 0.7 fusion.6
  86.4 0.9 copy.36.col_side_ref
  88.8 0.7 reshape.189.coef_ref
  89.5 1.4 copy-done.2
  90.9 2.5 %add.116 = f32[2,1024,256]{2,1,0:T(8,128)S(1)} add(f32[2,1024,256]{2,1,0:T(8,128)} %get-tuple-element.14, f32[2,1024,256]{2,1,0:T(8,128)} %copy-done.2) | non-fusion elementwise | flops 524288 | bytes 6291456 | tf_op jit(solution)/shard_map/add | solution.py:148
  93.5 1.6 collective-permute-start.1
  95.0 2.1 %sort.17 = (pred[64]{0:T(512)(128)(4,1)}, s32[64]{0:T(128)S(1)}) sort(pred[64]{0:T(512)(128)(4,1)S(1)} %compare_not_fusion, s32[64]{0:T(128)S(1)} %iota.46), dimensions={0}, to_apply=%region_3.4 | sort | flops 384 | bytes 640 | tf_op jit(solution)/shard_map/jit(argsort)/sort | solution.py:121
  97.1 0.7 pad_maximum_fusion
  98.6 20.6 %collective-permute-done.1 = f32[1,1024,256]{2,1,0:T(8,128)} collective-permute-done((f32[1,1024,256]{2,1,0:T(8,128)S(1)}, f32[1,1024,256]{2,1,0:T(8,128)}, u32[]{:S(2)}, u32[]{:S(2)}) %collective-permute-start.1) | collective-permute-done | bytes 1048608 | tf_op jit(solution)/shard_map/ppermute | solution.py:148
  119.2 1.4 fusion.9
  120.6 3.2 %all-to-all-done.1 = bf16[8,8,128,128]{3,2,1,0:T(8,128)(2,1)} async-done(((bf16[8,8,128,128]{3,2,1,0:T(8,128)(2,1)}), bf16[8,8,128,128]{3,2,1,0:T(8,128)(2,1)}, u32[]{:S(2)}, u32[]{:S(2)}) %all-to-all-start.1) | async-done | bytes 2097184 | tf_op jit(solution)/shard_map/all_to_all | solution.py:238
  123.8 2.5 %gather_fusion.2 = bf16[64,128,128]{2,1,0:T(8,128)(2,1)S(1)} fusion(bf16[64,128,128]{2,1,0:T(8,128)(2,1)} %bitcast.12, s32[1024]{0:T(1024)S(1)} %pad_clamp_fusion.1), kind=kCustom, calls=%fused_computation.2 | custom fusion | bytes 4194560 | tf_op jit(solution)/shard_map/jit(_take)/gather | solution.py:133
  126.4 1.6 broadcast_select_fusion.img_ref
  127.9 14.2 %shard_map.95 = (f32[2,1032,256]{2,1,0:T(8,128)}, f32[2,1032,256]{2,1,0:T(8,128)}) custom-call(s32[64]{0:T(128)} %copy-done.6, s32[1]{0:T(128)} %bitcast.10.count_ref, s32[64]{0:T(128)} %get-tuple-element.38.row_ref, s32[64]{0:T(128)} %get-tuple-element.44.group_ref, s32[64]{0:T(128)} %get-tuple-element.34.sub_ref, f32[64]{0:T(128)} %copy-done.4, ...), custom_call_target="tpu_custom_call" | custom-call | flops 4831838208 | bytes 6324224 | tf_op jit(solution)/shard_map/pallas_call | solution.py:123
  142.1 4.4 %collective-permute-done.2 = f32[2,1032,256]{2,1,0:T(8,128)S(1)} collective-permute-done((f32[2,1032,256]{2,1,0:T(8,128)}, f32[2,1032,256]{2,1,0:T(8,128)S(1)}, u32[]{:S(2)}, u32[]{:S(2)}) %collective-permute-start.2) | collective-permute-done | bytes 2113568 | tf_op jit(solution)/shard_map/ppermute | solution.py:148
  146.5 1.9 %add.121 = f32[2,1032,256]{2,1,0:T(8,128)S(1)} add(f32[2,1032,256]{2,1,0:T(8,128)} %get-tuple-element.18, f32[2,1032,256]{2,1,0:T(8,128)S(1)} %collective-permute-done.2) | non-fusion elementwise | flops 528384 | bytes 6340608 | tf_op jit(solution)/shard_map/add | solution.py:148
  148.5 0.9 collective-permute-start.3
  149.4 24.6 %collective-permute-done.3 = f32[1,1032,256]{2,1,0:T(8,128)S(1)} collective-permute-done((f32[1,1032,256]{2,1,0:T(8,128)S(1)}, f32[1,1032,256]{2,1,0:T(8,128)S(1)}, u32[]{:S(2)}, u32[]{:S(2)}) %collective-permute-start.3) | collective-permute-done | bytes 1056800 | tf_op jit(solution)/shard_map/ppermute | solution.py:148
  176.7 1.7 fusion.8
  (71 shorter events, 9.9 us)
Async XLA Ops:
  0.6 83.0 %copy-start = (bf16[9,41]{1,0:T(8,128)(2,1)S(1)}, bf16[9,41]{1,0:T(8,128)(2,1)}, u32[]{:S(2)}) copy-start(bf16[9,41]{1,0:T(8,128)(2,1)} %param.12) | copy-start | bytes 2218
  8.0 61.1 %all-to-all-start = ((bf16[8,8,144,128]{3,2,1,0:T(8,128)(2,1)}), bf16[8,8,144,128]{3,2,1,0:T(8,128)(2,1)S(1)}, u32[]{:S(2)}, u32[]{:S(2)}) async-start(bf16[8,8,144,128]{3,2,1,0:T(8,128)(2,1)} %bitcast.60), calls=%async_computation | async-start | bytes 4718592 | tf_op jit(solution)/shard_map/all_to_all | solution.py:198
  69.1 2.5 %copy-start.1 = (bf16[8,8,144,128]{3,2,1,0:T(8,128)(2,1)}, bf16[8,8,144,128]{3,2,1,0:T(8,128)(2,1)S(1)}, u32[]{:S(2)}) copy-start(bf16[8,8,144,128]{3,2,1,0:T(8,128)(2,1)S(1)} %all-to-all-done) | copy-start | bytes 7077892
  71.1 16.4 %copy-start.4 = (f32[64]{0:T(128)}, f32[64]{0:T(128)S(1)}, u32[]{:S(2)}) copy-start(f32[64]{0:T(128)S(1)} %get-tuple-element.33.w_ref) | copy-start | bytes 772
  71.6 52.2 %all-to-all-start.1 = ((bf16[8,8,128,128]{3,2,1,0:T(8,128)(2,1)}), bf16[8,8,128,128]{3,2,1,0:T(8,128)(2,1)}, u32[]{:S(2)}, u32[]{:S(2)}) async-start(bf16[8,8,128,128]{3,2,1,0:T(8,128)(2,1)} %bitcast.61), calls=%async_computation.1 | async-start | bytes 4194304 | tf_op jit(solution)/shard_map/all_to_all | solution.py:238
  77.2 8.4 %copy-start.5 = (bf16[9,41]{1,0:T(8,128)(2,1)S(1)}, bf16[9,41]{1,0:T(8,128)(2,1)}, u32[]{:S(2)}) copy-start(bf16[9,41]{1,0:T(8,128)(2,1)} %param.13) | copy-start | bytes 2218
  83.6 5.9 %collective-permute-start = (f32[2,1024,256]{2,1,0:T(8,128)}, f32[2,1024,256]{2,1,0:T(8,128)S(1)}, u32[]{:S(2)}, u32[]{:S(2)}) collective-permute-start(f32[2,1024,256]{2,1,0:T(8,128)} %get-tuple-element.15), channel_id=1, source_target_pairs={{0,1},{1,0},{2,3},{3,2},{4,5},{5,4},{6,7},{7,6},{8,9},{9,8},{10,11... | collective-permute-start | bytes 6291464 | tf_op jit(solution)/shard_map/ppermute | solution.py:148
  89.5 1.4 copy-start.2
  93.4 1.6 copy-start.3
  93.5 25.7 %collective-permute-start.1 = (f32[1,1024,256]{2,1,0:T(8,128)S(1)}, f32[1,1024,256]{2,1,0:T(8,128)}, u32[]{:S(2)}, u32[]{:S(2)}) collective-permute-start(f32[1,1024,256]{2,1,0:T(8,128)S(1)} %slice.70), channel_id=1, source_target_pairs={{0,2},{1,3},{2,0},{3,1},{4,6},{5,7},{6,4},{7,5},{8,10},{9,11},{10,... | collective-permute-start | bytes 3145736 | tf_op jit(solution)/shard_map/ppermute | solution.py:148
  97.1 29.2 %copy-start.6 = (s32[64]{0:T(128)}, s32[64]{0:T(128)S(1)}, u32[]{:S(2)}) copy-start(s32[64]{0:T(128)S(1)} %get-tuple-element.13.order_ref) | copy-start | bytes 772
  142.1 4.4 %collective-permute-start.2 = (f32[2,1032,256]{2,1,0:T(8,128)}, f32[2,1032,256]{2,1,0:T(8,128)S(1)}, u32[]{:S(2)}, u32[]{:S(2)}) collective-permute-start(f32[2,1032,256]{2,1,0:T(8,128)} %get-tuple-element.19), channel_id=1, source_target_pairs={{0,1},{1,0},{2,3},{3,2},{4,5},{5,4},{6,7},{7,6},{8,9},{9,8},{10,11... | collective-permute-start | bytes 6340616 | tf_op jit(solution)/shard_map/ppermute | solution.py:148
  148.5 25.4 %collective-permute-start.3 = (f32[1,1032,256]{2,1,0:T(8,128)S(1)}, f32[1,1032,256]{2,1,0:T(8,128)S(1)}, u32[]{:S(2)}, u32[]{:S(2)}) collective-permute-start(f32[1,1032,256]{2,1,0:T(8,128)S(1)} %slice.72), channel_id=1, source_target_pairs={{0,2},{1,3},{2,0},{3,1},{4,6},{5,7},{6,4},{7,5},{8,10},{9,11},{10,... | collective-permute-start | bytes 3170312 | tf_op jit(solution)/shard_map/ppermute | solution.py:148
